TPU v7x, 256 devices: a whole 4x4x8 slice. The times are simulated.
256 devices in a mesh: cells: 16 (over z, core), tracer: 16 (over y, x).
Axes of the slice: x: 4, y: 4, z: 8, core: 2. Of those that a mesh axis runs over, the one named last changes fastest.
Arguments:
- adjoint: float32 [64, 65536], P('tracer', 'cells'), may hold values from -6 to 6
- blocks: float32 [2048, 128, 128], P('cells'), may hold values from -0.375 to 0.375
- row_ptr: int32 [16, 33], P('cells'), may hold values from 0 to 128, as said below
- col_idx: int32 [2048], P('cells'), may hold values from 0 to 511, as said below
- regime: int32 [512], P('cells'), may hold values from 0 to 7
- jac: float32 [8, 64, 64], replicated, as said below
Outputs:
- sensitivity: float32 [64, 65536], P('tracer', 'cells')
Inputs may be any that keep to these rules, and one draw needn't show every extreme that they name: row_ptr[d, 0] = 0 and each block row holds 1 to 4 slots; some index of cells uses all 128 slots. `col_idx`: the first slot of each block row is its diagonal block; a live slot's column lies at most 32 blocks away from its block row, counted cyclically over the 512 blocks, and that distance is reached; slots past row_ptr[d, 32] hold any valid column. `jac`: each regime's matrix has diagonal entries of order one and off-diagonal couplings of order 0.1 between every pair of species.
All inputs are finite; a program needn't handle non-finite values.
Results may differ from a plain program's by a relative error of at most 0.0001.
Values sent between devices are 32-bit elements; how exact they have to be, the bound alone decides.
No kernel may reach another device: no remote copies, remote signals or barrier semaphores. Data moves between devices by JAX's collectives and lax.ppermute only.
A program may use at most 64 MiB of HBM per device.

v0:
```python
import jax
import jax.numpy as jnp
from jax import lax
from jax.sharding import PartitionSpec as P

BLOCK = 128
STEPS = 2


def with_halo(cells, sides, width):
    for axis, dim in sides:
        count = lax.axis_size(axis)
        head = lax.slice_in_dim(cells, 0, width, axis=dim)
        tail = lax.slice_in_dim(cells, cells.shape[dim] - width, cells.shape[dim], axis=dim)
        cells = jnp.concatenate(
            [
                lax.ppermute(tail, axis, [(i, (i + 1) % count) for i in range(count)]),
                cells,
                lax.ppermute(head, axis, [((i + 1) % count, i) for i in range(count)]),
            ],
            axis=dim,
        )
    return cells


def chemistry(moved, cell_regime, jac_table):
    result = jnp.zeros((jac_table.shape[2], moved.shape[1]), jnp.float32)
    for regime_id in range(jac_table.shape[0]):
        reacted = jnp.einsum(
            "ts,tc->sc", jac_table[regime_id], moved, precision=lax.Precision.HIGHEST
        )
        result = result + jnp.where(
            cell_regime[None, :] == regime_id, reacted, jnp.zeros_like(reacted)
        )
    return result


def body(adjoint, blocks, row_ptr, col_idx, regime, jac):
    spec_dev, cells_dev = adjoint.shape
    nb_dev = cells_dev // BLOCK
    cell_devices = lax.axis_size("cells")
    cell_index = lax.axis_index("cells")
    tracer_index = lax.axis_index("tracer")
    nb_total = nb_dev * cell_devices
    pointers = row_ptr[0]
    slot_count = blocks.shape[0]
    slot_ids = jnp.arange(slot_count)
    member = (
        (slot_ids[None, :] >= pointers[:-1, None]) & (slot_ids[None, :] < pointers[1:, None])
    ).astype(jnp.float32)
    live_slot = slot_ids < pointers[-1]
    local_col = jnp.mod(col_idx - (cell_index - 1) * nb_dev, nb_total)
    local_col = jnp.where(live_slot, local_col, 0)
    cell_regime = jnp.repeat(regime, BLOCK)
    adjoint_field = adjoint
    for hour_step in range(STEPS):
        extended = with_halo(adjoint_field, (("cells", 1),), cells_dev)
        extended_blocks = extended.reshape(spec_dev, 3 * nb_dev, BLOCK)
        picked = jnp.take(extended_blocks, local_col, axis=1, mode="clip")
        picked = jnp.where(live_slot[None, :, None], picked, jnp.zeros_like(picked))
        products = jnp.einsum("sij,qsj->qsi", blocks, picked, precision=lax.Precision.HIGHEST)
        moved = jnp.einsum(
            "rs,qsi->qri", member, products, precision=lax.Precision.HIGHEST
        ).reshape(spec_dev, cells_dev)
        whole = lax.all_gather(moved, "tracer", axis=0, tiled=True)
        species_rows = lax.dynamic_slice_in_dim(jac, tracer_index * spec_dev, spec_dev, 2)
        adjoint_field = chemistry(whole, cell_regime, species_rows)
    return adjoint_field


def solution(mesh):
    return jax.shard_map(
        body,
        mesh=mesh,
        in_specs=(
            P("tracer", "cells"),
            P("cells", None, None),
            P("cells", None),
            P("cells"),
            P("cells"),
            P(),
        ),
        out_specs=P("tracer", "cells"),
        check_vma=False,
    )
```

profile of v0, /device:TPU:2, one launch (start us, length us, event | category | flops | bytes accessed | tf_op | source)
XLA Modules:
  0.0 172.9 jit_solution(1758554243512436759)
XLA Ops:
  6.5 0.0 copy-start
  6.5 0.0 copy-start.1
  6.5 0.0 all-gather.5.cloned.1.call-start
  6.5 0.0 collective-permute-start
  6.6 5.3 %collective-permute-start.1 = (f32[4,4096]{1,0:T(4,128)}, f32[4,4096]{1,0:T(4,128)S(1)}, u32[]{:S(2)}, u32[]{:S(2)}) collective-permute-start(f32[4,4096]{1,0:T(4,128)} %param.6), channel_id=1, source_target_pairs={{16,0},{32,16},{48,32},{64,48},{80,64},{96,80},{112,96},{128,112},... | collective-permute-start | bytes 196616 | tf_op jit(solution)/shard_map/ppermute | solution.py:19
  11.9 1.2 slice.45
  13.1 0.8 slice_bitcast_fusion.1
  13.9 1.3 fusion.48
  15.2 0.7 iota_compare_fusion.2
  15.9 0.0 collective-permute-done
  15.9 0.0 collective-permute-done.1
  15.9 0.9 maximum_bitcast_fusion
  16.8 0.7 gather_fusion
  17.5 15.5 %convolution_bitcast_fusion.1 = f32[4,128,128]{2,0,1:T(4,128)S(1)} fusion(f32[128,128,128]{2,1,0:T(8,128)} %param.7, f32[128,4,128]{2,1,0:T(4,128)S(1)} %gather_fusion, pred[128]{0:T(512)(128)(4,1)S(1)} %iota_compare_fusion.2), kind=kOutput, calls=%fused_computation.33 | convolution fusion | flops 100728832 | bytes 8913024 | tf_op jit(solution)/shard_map/sij,qsj->qsi/dot_general | solution.py:61
  33.0 0.2 convolution_bitcast_fusion.3
  33.3 0.7 reshape.118
  33.9 0.0 all-gather.5.cloned.1.call-update
  34.0 0.0 all-gather.7.cloned.1.call-start
  34.0 0.0 copy-done.1
  34.0 0.1 broadcast_bitcast_fusion.6
  34.1 0.1 broadcast_bitcast_fusion.4
  34.2 0.1 broadcast_bitcast_fusion.2
  34.3 0.1 broadcast_bitcast_fusion
  34.4 47.5 %all-gather.5.cloned.1.call-done = f32[16,4,4096]{2,1,0:T(4,128)} async-done(((f32[1,4,4096]{2,1,0:T(4,128)}), f32[16,4,4096]{2,1,0:T(4,128)}) %all-gather.5.cloned.1.call-update) | async-done | bytes 1048592 | tf_op jit(solution)/shard_map/all_gather | solution.py:65
  81.8 1.6 reshape.119
  83.4 0.0 copy-done
  83.4 0.7 convolution_select_fusion.15
  84.1 0.7 fusion.13
  84.8 0.7 fusion.12
  85.5 0.7 fusion.11
  86.1 0.7 fusion.10
  86.8 0.7 fusion.9
  87.5 0.7 fusion.8
  88.1 0.7 fusion.7
  88.8 0.0 collective-permute-start.2
  88.8 2.9 %collective-permute-start.3 = (f32[4,4096]{1,0:T(4,128)S(1)}, f32[4,4096]{1,0:T(4,128)S(1)}, u32[]{:S(2)}, u32[]{:S(2)}) collective-permute-start(f32[4,4096]{1,0:T(4,128)S(1)} %fusion.7), channel_id=1, source_target_pairs={{16,0},{32,16},{48,32},{64,48},{80,64},{96,80},{112,96},{128,112},... | collective-permute-start | bytes 196616 | tf_op jit(solution)/shard_map/ppermute | solution.py:19
  91.8 1.9 %collective-permute-done.2 = f32[4,4096]{1,0:T(4,128)S(1)} collective-permute-done((f32[4,4096]{1,0:T(4,128)S(1)}, f32[4,4096]{1,0:T(4,128)S(1)}, u32[]{:S(2)}, u32[]{:S(2)}) %collective-permute-start.2) | collective-permute-done | bytes 65568 | tf_op jit(solution)/shard_map/ppermute | solution.py:17
  93.7 0.0 collective-permute-done.3
  93.8 0.7 gather_fusion.1
  94.5 15.7 %convolution_bitcast_fusion = f32[4,128,128]{2,0,1:T(4,128)S(1)} fusion(f32[128,128,128]{2,1,0:T(8,128)} %param.7, f32[128,4,128]{2,1,0:T(4,128)S(1)} %gather_fusion.1, pred[128]{0:T(512)(128)(4,1)S(1)} %iota_compare_fusion.2), kind=kOutput, calls=%fused_computation.32 | convolution fusion | flops 100728832 | bytes 8913024 | tf_op jit(solution)/shard_map/sij,qsj->qsi/dot_general | solution.py:61
  110.2 0.2 convolution_bitcast_fusion.2
  110.5 0.7 reshape.120
  111.1 0.0 all-gather.7.cloned.1.call-update
  111.1 47.4 %all-gather.7.cloned.1.call-done = f32[16,4,4096]{2,1,0:T(4,128)} async-done(((f32[1,4,4096]{2,1,0:T(4,128)}), f32[16,4,4096]{2,1,0:T(4,128)}) %all-gather.7.cloned.1.call-update) | async-done | bytes 1048592 | tf_op jit(solution)/shard_map/all_gather | solution.py:65
  158.5 1.6 reshape.121
  160.1 0.7 convolution_select_fusion.7
  160.8 0.7 fusion.6
  161.4 0.7 fusion.5
  162.1 0.7 fusion.4
  162.8 0.7 fusion.3
  163.5 0.7 fusion.2
  164.1 0.7 fusion.1
  164.8 1.3 fusion
  (3 shorter events, 0.1 us)
Async XLA Ops:
  6.5 76.9 %copy-start = (f32[8,64,64]{2,1,0:T(8,128)S(1)}, f32[8,64,64]{2,1,0:T(8,128)}, u32[]{:S(2)}) copy-start(f32[8,64,64]{2,1,0:T(8,128)} %param.11) | copy-start | bytes 393220
  6.5 27.5 %copy-start.1 = (s32[32]{0:T(128)S(1)}, s32[32]{0:T(128)}, u32[]{:S(2)}) copy-start(s32[32]{0:T(128)} %param.10) | copy-start | bytes 388
  6.5 75.3 %all-gather.5.cloned.1.call-start = ((), (), s32[]{:S(2)}) async-start(), calls=%async_computation | async-start | bytes 1114112 | tf_op jit(solution)/shard_map/all_gather | solution.py:65
  6.5 9.3 %collective-permute-start = (f32[4,4096]{1,0:T(4,128)}, f32[4,4096]{1,0:T(4,128)S(1)}, u32[]{:S(2)}, u32[]{:S(2)}) collective-permute-start(f32[4,4096]{1,0:T(4,128)} %param.6), channel_id=1, source_target_pairs={{0,16},{16,32},{32,48},{48,64},{64,80},{80,96},{96,112},{112,128},... | collective-permute-start | bytes 196616 | tf_op jit(solution)/shard_map/ppermute | solution.py:17
  6.6 9.3 %collective-permute-start.1 = (f32[4,4096]{1,0:T(4,128)}, f32[4,4096]{1,0:T(4,128)S(1)}, u32[]{:S(2)}, u32[]{:S(2)}) collective-permute-start(f32[4,4096]{1,0:T(4,128)} %param.6), channel_id=1, source_target_pairs={{16,0},{32,16},{48,32},{64,48},{80,64},{96,80},{112,96},{128,112},... | collective-permute-start | bytes 196616 | tf_op jit(solution)/shard_map/ppermute | solution.py:19
  34.0 124.5 %all-gather.7.cloned.1.call-start = ((), (), s32[]{:S(2)}) async-start(), calls=%async_computation.1 | async-start | bytes 1114112 | tf_op jit(solution)/shard_map/all_gather | solution.py:65
  88.8 4.9 %collective-permute-start.2 = (f32[4,4096]{1,0:T(4,128)S(1)}, f32[4,4096]{1,0:T(4,128)S(1)}, u32[]{:S(2)}, u32[]{:S(2)}) collective-permute-start(f32[4,4096]{1,0:T(4,128)S(1)} %fusion.7), channel_id=1, source_target_pairs={{0,16},{16,32},{32,48},{48,64},{64,80},{80,96},{96,112},{112,128},... | collective-permute-start | bytes 196616 | tf_op jit(solution)/shard_map/ppermute | solution.py:17
  88.8 4.9 %collective-permute-start.3 = (f32[4,4096]{1,0:T(4,128)S(1)}, f32[4,4096]{1,0:T(4,128)S(1)}, u32[]{:S(2)}, u32[]{:S(2)}) collective-permute-start(f32[4,4096]{1,0:T(4,128)S(1)} %fusion.7), channel_id=1, source_target_pairs={{16,0},{32,16},{48,32},{64,48},{80,64},{96,80},{112,96},{128,112},... | collective-permute-start | bytes 196616 | tf_op jit(solution)/shard_map/ppermute | solution.py:19
Sparse Core Ops, SparseCore 0:
  34.1 47.7 all-gather.4
  111.3 47.1 all-gather.6
where the time goes:
time: 173 us
  waiting for transfers between devices  96.8 us (56%)
  matrix products  42.9 us (25%)
  between operations  13.6 us (8%)
  local copies, waits for them, and re-layouts  8.34 us (5%)
  starting transfers between devices  8.32 us (5%)
  other arithmetic  2.91 us (2%)
    all_gather x2, waiting for transfers between devices, body(): whole = lax.all_gather(moved, 'tracer', axis=0, tiled=True)  94.9 us
    dot_general x2, matrix products, body(): jnp.einsum('sij,qsj->qsi', blocks, picked, precision=lax.Precision.HIGHEST)  31.2 us
    dot_general x16, matrix products, chemistry(): jnp.einsum('ts,tc->sc', jac_table[regime_id], moved, precision=lax.Precis...  11.3 us
    ppermute x2, starting transfers between devices, with_halo(): lax.ppermute(head, axis, [((i + 1) % count, i) for i in range(count)])  8.25 us
    unnamed x8, local copies, waits for them, and re-layouts  4.5 us
  transfers between devices with their start and end apart: 6, of which 3 were waited for; matrix products, arithmetic and copies ran while one was open for 2% of the time, Pallas kernels for 0%

commit v1 on v0

--- a/solution.py
+++ b/solution.py
@@ -23,16 +23,12 @@
     return cells
 
 
-def chemistry(moved, cell_regime, jac_table):
-    result = jnp.zeros((jac_table.shape[2], moved.shape[1]), jnp.float32)
-    for regime_id in range(jac_table.shape[0]):
-        reacted = jnp.einsum(
-            "ts,tc->sc", jac_table[regime_id], moved, precision=lax.Precision.HIGHEST
-        )
-        result = result + jnp.where(
-            cell_regime[None, :] == regime_id, reacted, jnp.zeros_like(reacted)
-        )
-    return result
+def chemistry_local(moved, block_jac):
+    spec, cells = moved.shape
+    nblk = cells // BLOCK
+    per_block = moved.reshape(spec, nblk, BLOCK)
+    out = jnp.einsum("but,ubc->tbc", block_jac, per_block, precision=lax.Precision.HIGHEST)
+    return out.reshape(spec, cells)
 
 
 def body(adjoint, blocks, row_ptr, col_idx, regime, jac):
@@ -40,6 +36,7 @@
     nb_dev = cells_dev // BLOCK
     cell_devices = lax.axis_size("cells")
     cell_index = lax.axis_index("cells")
+    tracer_devices = lax.axis_size("tracer")
     tracer_index = lax.axis_index("tracer")
     nb_total = nb_dev * cell_devices
     pointers = row_ptr[0]
@@ -51,7 +48,9 @@
     live_slot = slot_ids < pointers[-1]
     local_col = jnp.mod(col_idx - (cell_index - 1) * nb_dev, nb_total)
     local_col = jnp.where(live_slot, local_col, 0)
-    cell_regime = jnp.repeat(regime, BLOCK)
+    own_blocks = nb_dev // tracer_devices
+    own_regime = lax.dynamic_slice_in_dim(regime, tracer_index * own_blocks, own_blocks)
+    block_jac = jnp.take(jac, own_regime, axis=0)
     adjoint_field = adjoint
     for hour_step in range(STEPS):
         extended = with_halo(adjoint_field, (("cells", 1),), cells_dev)
@@ -62,9 +61,9 @@
         moved = jnp.einsum(
             "rs,qsi->qri", member, products, precision=lax.Precision.HIGHEST
         ).reshape(spec_dev, cells_dev)
-        whole = lax.all_gather(moved, "tracer", axis=0, tiled=True)
-        species_rows = lax.dynamic_slice_in_dim(jac, tracer_index * spec_dev, spec_dev, 2)
-        adjoint_field = chemistry(whole, cell_regime, species_rows)
+        split = lax.all_to_all(moved, "tracer", 1, 0, tiled=True)
+        reacted = chemistry_local(split, block_jac)
+        adjoint_field = lax.all_to_all(reacted, "tracer", 0, 1, tiled=True)
     return adjoint_field
 
 

time: 173 us -> 98.3 us (0.57)
  waiting for transfers between devices: 96.8 us -> 10.5 us
  blocking collectives: 0 us -> 32.4 us
  between operations: 13.6 us -> 0.15 us
  matrix products: 42.9 us -> 32.1 us
  starting transfers between devices: 8.32 us -> 13.3 us
  local copies, waits for them, and re-layouts: 8.34 us -> 5.82 us
    all_gather x2 -> x0, waiting for transfers between devices: 94.9 us -> none  [body(): whole = lax.all_gather(moved, 'tracer', axis=0, tiled=True)]
    all_to_all x0 -> x3, blocking collectives: none -> 32.4 us  [the longest x2 21.6 us: body(): adjoint_field = lax.all_to_all(reacted, 'tracer', 0, 1, tiled=True)]
    dot_general x16 -> x2, matrix products: 11.3 us -> 0.75 us  [chemistry_local(): jnp.einsum('but,ubc->tbc', block_jac, per_block, precision=lax.Precision....]
    all_to_all x0 -> x1, starting transfers between devices: none -> 7.48 us  [body(): split = lax.all_to_all(moved, 'tracer', 1, 0, tiled=True)]
    all_to_all x0 -> x1, waiting for transfers between devices: none -> 5.73 us  [body(): split = lax.all_to_all(moved, 'tracer', 1, 0, tiled=True)]
    unnamed x8 -> x3, local copies, waits for them, and re-layouts: 4.5 us -> 0.63 us
    ppermute x2, starting transfers between devices: 8.25 us -> 5.32 us  [with_halo(): lax.ppermute(head, axis, [((i + 1) % count, i) for i in range(count)])]
  transfers between devices with their start and end apart: 6 -> 5, of which waited for: 3 -> 4; matrix products, arithmetic and copies ran while one was open for 2% -> 5% of each run, Pallas kernels for 0% -> 0%
where the time goes in v1:
time: 98.3 us; the launch traced here: 97.9 us
  blocking collectives  32.4 us (33%)
  matrix products  32.1 us (33%)
  starting transfers between devices  13.3 us (14%)
  waiting for transfers between devices  10.5 us (11%)
  local copies, waits for them, and re-layouts  5.82 us (6%)
  other arithmetic  3.64 us (4%)
    dot_general x2, matrix products, body(): jnp.einsum('sij,qsj->qsi', blocks, picked, precision=lax.Precision.HIGHEST)  30.9 us
    all_to_all x2, blocking collectives, body(): adjoint_field = lax.all_to_all(reacted, 'tracer', 0, 1, tiled=True)  21.6 us
    all_to_all x1, blocking collectives, body(): split = lax.all_to_all(moved, 'tracer', 1, 0, tiled=True)  10.8 us
    all_to_all x1, starting transfers between devices, body(): split = lax.all_to_all(moved, 'tracer', 1, 0, tiled=True)  7.48 us
    all_to_all x1, waiting for transfers between devices, body(): split = lax.all_to_all(moved, 'tracer', 1, 0, tiled=True)  5.73 us
    ppermute x2, starting transfers between devices, with_halo(): lax.ppermute(head, axis, [((i + 1) % count, i) for i in range(count)])  5.32 us
    ppermute x2, waiting for transfers between devices, with_halo(): lax.ppermute(tail, axis, [(i, (i + 1) % count) for i in range(count)])  3.34 us
  transfers between devices with their start and end apart: 5, of which 4 were waited for; matrix products, arithmetic and copies ran while one was open for 5% of the time, Pallas kernels for 0%

profile of v1, /device:TPU:2, one launch (start us, length us, event | category | flops | bytes accessed | tf_op | source)
XLA Modules:
  0.0 97.9 jit_solution(14518944231402138821)
XLA Ops:
  0.0 0.0 copy-start
  0.0 5.3 %collective-permute-start.1 = (f32[4,4096]{1,0:T(4,128)}, f32[4,4096]{1,0:T(4,128)S(1)}, u32[]{:S(2)}, u32[]{:S(2)}) collective-permute-start(f32[4,4096]{1,0:T(4,128)} %param.6), channel_id=1, source_target_pairs={{16,0},{32,16},{48,32},{64,48},{80,64},{96,80},{112,96},{128,112},... | collective-permute-start | bytes 196616 | tf_op jit(solution)/shard_map/ppermute | solution.py:19
  5.3 0.0 collective-permute-start
  5.3 1.2 %slice.12 = s32[1,1]{1,0:T(1,128)} slice(s32[1,33]{1,0:T(1,128)} %param.8), slice={[0:1], [32:33]} | slice | bytes 8 | tf_op jit(solution)/shard_map/slice | solution.py:48
  6.5 0.8 slice_bitcast_fusion.1
  7.3 1.3 %fusion.30 = s32[128]{0:T(128)S(1)} fusion(s32[128]{0:T(128)} %param.9, s32[]{:T(128)S(6)} %mul.6, s32[]{:T(128)} %bitcast), kind=kLoop, calls=%fused_computation.46 | loop fusion | flops 1792 | bytes 1032 | tf_op jit(solution)/shard_map/jit(_where)/select_n | solution.py:50
  8.7 0.7 compare_and_fusion
  9.4 0.6 iota_compare_fusion.2
  10.1 0.0 collective-permute-done.1
  10.1 0.3 collective-permute-done
  10.4 0.9 maximum_bitcast_fusion
  11.3 0.7 gather_fusion
  12.1 15.5 %fusion.4 = f32[128,4,128]{2,1,0:T(4,128)S(1)} fusion(f32[128,128,128]{2,1,0:T(8,128)} %param.7, f32[128,4,128]{2,1,0:T(4,128)S(1)} %gather_fusion, pred[128]{0:T(512)(128)(4,1)S(1)} %iota_compare_fusion.2), kind=kOutput, calls=%fused_computation.11 | convolution fusion | flops 100728832 | bytes 8913024 | tf_op jit(solution)/shard_map/sij,qsj->qsi/dot_general | solution.py:60
  27.5 0.2 convolution_bitcast_fusion.3
  27.8 0.7 copy.9
  28.5 7.5 %all-to-all-start = ((f32[4,16,256]{2,0,1:T(4,128)}), f32[4,16,256]{2,0,1:T(4,128)S(1)}, u32[]{:S(2)}, u32[]{:S(2)}) async-start(f32[4,16,256]{2,0,1:T(4,128)} %copy.9), calls=%async_computation | async-start | bytes 131072 | tf_op jit(solution)/shard_map/all_to_all | solution.py:64
  36.0 0.0 copy-done
  36.0 0.6 gather_fusion.1
  36.5 5.7 %all-to-all-done = f32[4,16,256]{2,0,1:T(4,128)S(1)} async-done(((f32[4,16,256]{2,0,1:T(4,128)}), f32[4,16,256]{2,0,1:T(4,128)S(1)}, u32[]{:S(2)}, u32[]{:S(2)}) %all-to-all-start) | async-done | bytes 65568 | tf_op jit(solution)/shard_map/all_to_all | solution.py:64
  42.3 0.4 convolution_bitcast_fusion.2
  42.7 0.1 copy.12
  42.7 0.1 all_to_all.55
  42.8 10.8 %all_to_all.70 = f32[16,4,256]{2,1,0:T(4,128)S(1)} all-to-all(f32[16,4,256]{2,1,0:T(4,128)S(1)} %all_to_all.55), channel_id=1, replica_groups=mesh['cells'=16,'tracer'=16] {'tracer'}, dimensions={0} | all-to-all | bytes 131072 | tf_op jit(solution)/shard_map/all_to_all | solution.py:66
  53.6 0.0 collective-permute-start.3
  53.6 0.5 collective-permute-start.2
  54.1 1.4 %collective-permute-done.3 = f32[4,4096]{1,0:T(4,128)S(1)} collective-permute-done((f32[4,4096]{1,0:T(4,128)S(1)}, f32[4,4096]{1,0:T(4,128)S(1)}, u32[]{:S(2)}, u32[]{:S(2)}) %collective-permute-start.3) | collective-permute-done | bytes 65568 | tf_op jit(solution)/shard_map/ppermute | solution.py:19
  55.6 3.0 %collective-permute-done.2 = f32[4,4096]{1,0:T(4,128)S(1)} collective-permute-done((f32[4,4096]{1,0:T(4,128)S(1)}, f32[4,4096]{1,0:T(4,128)S(1)}, u32[]{:S(2)}, u32[]{:S(2)}) %collective-permute-start.2) | collective-permute-done | bytes 65568 | tf_op jit(solution)/shard_map/ppermute | solution.py:17
  58.6 0.7 gather_fusion.2
  59.3 15.5 %fusion.1 = f32[128,4,128]{2,1,0:T(4,128)S(1)} fusion(f32[128,128,128]{2,1,0:T(8,128)} %param.7, f32[128,4,128]{2,1,0:T(4,128)S(1)} %gather_fusion.2, pred[128]{0:T(512)(128)(4,1)S(1)} %iota_compare_fusion.2), kind=kOutput, calls=%fused_computation.8 | convolution fusion | flops 100728832 | bytes 8913024 | tf_op jit(solution)/shard_map/sij,qsj->qsi/dot_general | solution.py:60
  74.8 0.2 convolution_bitcast_fusion.1
  75.1 10.8 %all_to_all.71 = f32[4,16,256]{2,0,1:T(4,128)S(1)} all-to-all(f32[4,16,256]{2,0,1:T(4,128)S(1)} %copy.15), channel_id=1, replica_groups=mesh['cells'=16,'tracer'=16] {'tracer'}, dimensions={1} | all-to-all | bytes 131072 | tf_op jit(solution)/shard_map/all_to_all | solution.py:64
  86.0 0.4 convolution_bitcast_fusion
  86.4 0.1 copy.18
  86.4 0.1 all_to_all.62
  86.5 10.8 %all_to_all.72 = f32[16,4,256]{2,1,0:T(4,128)S(1)} all-to-all(f32[16,4,256]{2,1,0:T(4,128)S(1)} %all_to_all.62), channel_id=1, replica_groups=mesh['cells'=16,'tracer'=16] {'tracer'}, dimensions={0} | all-to-all | bytes 131072 | tf_op jit(solution)/shard_map/all_to_all | solution.py:66
  97.3 0.6 copy.36
  (8 shorter events, 0.2 us)
Async XLA Ops:
  0.0 36.0 %copy-start = (f32[8,64,64]{2,1,0:T(8,128)S(1)}, f32[8,64,64]{2,1,0:T(8,128)}, u32[]{:S(2)}) copy-start(f32[8,64,64]{2,1,0:T(8,128)} %param.11) | copy-start | bytes 393220
  0.0 10.1 %collective-permute-start.1 = (f32[4,4096]{1,0:T(4,128)}, f32[4,4096]{1,0:T(4,128)S(1)}, u32[]{:S(2)}, u32[]{:S(2)}) collective-permute-start(f32[4,4096]{1,0:T(4,128)} %param.6), channel_id=1, source_target_pairs={{16,0},{32,16},{48,32},{64,48},{80,64},{96,80},{112,96},{128,112},... | collective-permute-start | bytes 196616 | tf_op jit(solution)/shard_map/ppermute | solution.py:19
  5.3 5.1 %collective-permute-start = (f32[4,4096]{1,0:T(4,128)}, f32[4,4096]{1,0:T(4,128)S(1)}, u32[]{:S(2)}, u32[]{:S(2)}) collective-permute-start(f32[4,4096]{1,0:T(4,128)} %param.6), channel_id=1, source_target_pairs={{0,16},{16,32},{32,48},{48,64},{64,80},{80,96},{96,112},{112,128},... | collective-permute-start | bytes 196616 | tf_op jit(solution)/shard_map/ppermute | solution.py:17
  28.5 13.8 %all-to-all-start = ((f32[4,16,256]{2,0,1:T(4,128)}), f32[4,16,256]{2,0,1:T(4,128)S(1)}, u32[]{:S(2)}, u32[]{:S(2)}) async-start(f32[4,16,256]{2,0,1:T(4,128)} %copy.9), calls=%async_computation | async-start | bytes 131072 | tf_op jit(solution)/shard_map/all_to_all | solution.py:64
  53.6 1.9 %collective-permute-start.3 = (f32[4,4096]{1,0:T(4,128)S(1)}, f32[4,4096]{1,0:T(4,128)S(1)}, u32[]{:S(2)}, u32[]{:S(2)}) collective-permute-start(f32[4,4096]{1,0:T(4,128)S(1)} %bitcast.48), channel_id=1, source_target_pairs={{16,0},{32,16},{48,32},{64,48},{80,64},{96,80},{112,96},{128,112},... | collective-permute-start | bytes 196616 | tf_op jit(solution)/shard_map/ppermute | solution.py:19
  53.6 4.9 %collective-permute-start.2 = (f32[4,4096]{1,0:T(4,128)S(1)}, f32[4,4096]{1,0:T(4,128)S(1)}, u32[]{:S(2)}, u32[]{:S(2)}) collective-permute-start(f32[4,4096]{1,0:T(4,128)S(1)} %bitcast.49), channel_id=1, source_target_pairs={{0,16},{16,32},{32,48},{48,64},{64,80},{80,96},{96,112},{112,128},... | collective-permute-start | bytes 196616 | tf_op jit(solution)/shard_map/ppermute | solution.py:17

commit v2 on v1

--- a/solution.py
+++ b/solution.py
@@ -1,10 +1,75 @@
 import jax
 import jax.numpy as jnp
 from jax import lax
+from jax.experimental import pallas as pl
+from jax.experimental.pallas import tpu as pltpu
 from jax.sharding import PartitionSpec as P
 
 BLOCK = 128
 STEPS = 2
+ROWS_PER_STEP = 4
+KMAX = 4
+
+
+def transport_kernel(start_ref, off_ref, cnt_ref, col_ref, ext_ref, blk_ref, out_ref, acc_ref):
+    g = pl.program_id(0)
+    spec = ext_ref.shape[0]
+    window = blk_ref.shape[0]
+    n_ext = ext_ref.shape[1] // BLOCK
+    for rr in range(ROWS_PER_STEP):
+        r = g * ROWS_PER_STEP + rr
+        off = off_ref[r]
+        cnt = cnt_ref[r]
+        base = start_ref[g]
+        xs = []
+        for k in range(KMAX):
+            local = jnp.minimum(off + k, window - 1)
+            col = jnp.clip(col_ref[base + local], 0, n_ext - 1)
+            x = ext_ref[:, pl.ds(pl.multiple_of(col * BLOCK, BLOCK), BLOCK)]
+            x = jnp.where(k < cnt, x, jnp.zeros_like(x))
+            xs.append((local, x))
+        for ic in range(BLOCK // 32):
+            rows = slice(ic * 32, (ic + 1) * 32)
+            accs = [None] * spec
+            for local, x in xs:
+                b = blk_ref[local, rows, :]
+                for q in range(spec):
+                    term = b * x[q:q + 1, :]
+                    accs[q] = term if accs[q] is None else accs[q] + term
+            for q in range(spec):
+                acc_ref[q, rows, :] = accs[q]
+        for q in range(spec):
+            y = jnp.sum(acc_ref[q].T, axis=0, keepdims=True)
+            out_ref[q:q + 1, rr * BLOCK:(rr + 1) * BLOCK] = y
+
+
+def transport(ext, blocks, row_ptr, local_col):
+    spec = ext.shape[0]
+    slots = blocks.shape[0]
+    nrows = row_ptr.shape[0] - 1
+    groups = nrows // ROWS_PER_STEP
+    window = ROWS_PER_STEP * KMAX
+    starts = jnp.minimum(row_ptr[0:nrows:ROWS_PER_STEP], slots - window).astype(jnp.int32)
+    group_of_row = jnp.arange(nrows) // ROWS_PER_STEP
+    offs = (row_ptr[:-1] - starts[group_of_row]).astype(jnp.int32)
+    cnts = jnp.clip(row_ptr[1:] - row_ptr[:-1], 0, KMAX).astype(jnp.int32)
+    grid_spec = pltpu.PrefetchScalarGridSpec(
+        num_scalar_prefetch=4,
+        grid=(groups,),
+        in_specs=[
+            pl.BlockSpec(ext.shape, lambda g, s, o, c, l: (0, 0)),
+            pl.BlockSpec((pl.Element(window), pl.Element(BLOCK), pl.Element(BLOCK)), lambda g, s, o, c, l: (s[g], 0, 0)),
+        ],
+        out_specs=pl.BlockSpec((spec, ROWS_PER_STEP * BLOCK), lambda g, s, o, c, l: (0, g)),
+        scratch_shapes=[pltpu.VMEM((spec, BLOCK, BLOCK), jnp.float32)],
+    )
+    flops = 2 * slots * BLOCK * BLOCK * spec
+    return pl.pallas_call(
+        transport_kernel,
+        grid_spec=grid_spec,
+        out_shape=jax.ShapeDtypeStruct((spec, nrows * BLOCK), jnp.float32),
+        cost_estimate=pl.CostEstimate(flops=flops, bytes_accessed=blocks.size * 4 + ext.size * 4, transcendentals=0),
+    )(starts, offs, cnts, local_col.astype(jnp.int32), ext, blocks)
 
 
 def with_halo(cells, sides, width):
@@ -42,9 +107,6 @@
     pointers = row_ptr[0]
     slot_count = blocks.shape[0]
     slot_ids = jnp.arange(slot_count)
-    member = (
-        (slot_ids[None, :] >= pointers[:-1, None]) & (slot_ids[None, :] < pointers[1:, None])
-    ).astype(jnp.float32)
     live_slot = slot_ids < pointers[-1]
     local_col = jnp.mod(col_idx - (cell_index - 1) * nb_dev, nb_total)
     local_col = jnp.where(live_slot, local_col, 0)
@@ -54,13 +116,7 @@
     adjoint_field = adjoint
     for hour_step in range(STEPS):
         extended = with_halo(adjoint_field, (("cells", 1),), cells_dev)
-        extended_blocks = extended.reshape(spec_dev, 3 * nb_dev, BLOCK)
-        picked = jnp.take(extended_blocks, local_col, axis=1, mode="clip")
-        picked = jnp.where(live_slot[None, :, None], picked, jnp.zeros_like(picked))
-        products = jnp.einsum("sij,qsj->qsi", blocks, picked, precision=lax.Precision.HIGHEST)
-        moved = jnp.einsum(
-            "rs,qsi->qri", member, products, precision=lax.Precision.HIGHEST
-        ).reshape(spec_dev, cells_dev)
+        moved = transport(extended, blocks, pointers, local_col)
         split = lax.all_to_all(moved, "tracer", 1, 0, tiled=True)
         reacted = chemistry_local(split, block_jac)
         adjoint_field = lax.all_to_all(reacted, "tracer", 0, 1, tiled=True)

time: 98.3 us -> 85.3 us (0.87)
  matrix products: 32.1 us -> 0.75 us
  Pallas kernels: 0 us -> 17.1 us
  other arithmetic: 3.64 us -> 6.22 us
  local copies, waits for them, and re-layouts: 5.82 us -> 4.2 us
    dot_general x4 -> x0, matrix products: 31.4 us -> none  [the longest x2 30.9 us: body(): jnp.einsum('sij,qsj->qsi', blocks, picked, precision=lax.Precision.HIGHEST)]
    pallas_call x0 -> x2, Pallas kernels: none -> 17.1 us  [transport(): pl.pallas_call(transport_kernel, grid_spec=grid_spec, out_shape=jax.Shape...]
    concatenate x1 -> x2, other arithmetic: 0.04 us -> 2.27 us  [with_halo(): jnp.concatenate([lax.ppermute(tail, axis, [(i, (i + 1) % count) for i in...]
    min x0 -> x2, other arithmetic: none -> 1.36 us  [the longest x1 1.36 us: transport(): cnts = jnp.clip(row_ptr[1:] - row_ptr[:-1], 0, KMAX).astype(jnp.int32)]
  transfers between devices with their start and end apart: 5 -> 5, of which waited for: 4 -> 3; matrix products, arithmetic and copies ran while one was open for 5% -> 8% of each run, Pallas kernels for 0% -> 0%
where the time goes in v2:
time: 85.3 us; the launch traced here: 84.6 us
  blocking collectives  32.7 us (38%)
  Pallas kernels  17.1 us (20%)
  starting transfers between devices  13.3 us (16%)
  waiting for transfers between devices  10.1 us (12%)
  other arithmetic  6.22 us (7%)
  local copies, waits for them, and re-layouts  4.2 us (5%)
    all_to_all x2, blocking collectives, body(): adjoint_field = lax.all_to_all(reacted, 'tracer', 0, 1, tiled=True)  21.6 us
    pallas_call x2, Pallas kernels, transport(): pl.pallas_call(transport_kernel, grid_spec=grid_spec, out_shape=jax.Shape...  17.1 us
    all_to_all x1, blocking collectives, body(): split = lax.all_to_all(moved, 'tracer', 1, 0, tiled=True)  11.1 us
    all_to_all x1, starting transfers between devices, body(): split = lax.all_to_all(moved, 'tracer', 1, 0, tiled=True)  7.48 us
    all_to_all x1, waiting for transfers between devices, body(): split = lax.all_to_all(moved, 'tracer', 1, 0, tiled=True)  5.73 us
    ppermute x2, starting transfers between devices, with_halo(): lax.ppermute(head, axis, [((i + 1) % count, i) for i in range(count)])  5.31 us
    ppermute x2, waiting for transfers between devices, with_halo(): lax.ppermute(tail, axis, [(i, (i + 1) % count) for i in range(count)])  3 us
    concatenate x2, other arithmetic, with_halo(): jnp.concatenate([lax.ppermute(tail, axis, [(i, (i + 1) % count) for i in...  2.27 us
  transfers between devices with their start and end apart: 5, of which 3 were waited for; matrix products, arithmetic and copies ran while one was open for 8% of the time, Pallas kernels for 0%

profile of v2, /device:TPU:2, one launch (start us, length us, event | category | flops | bytes accessed | tf_op | source)
XLA Modules:
  0.0 84.6 jit_solution(11047402775723861325)
XLA Ops:
  0.0 0.0 copy-start
  0.0 0.0 collective-permute-start
  0.0 5.3 %collective-permute-start.1 = (f32[4,4096]{1,0:T(4,128)}, f32[4,4096]{1,0:T(4,128)S(1)}, u32[]{:S(2)}, u32[]{:S(2)}) collective-permute-start(f32[4,4096]{1,0:T(4,128)} %param.6), channel_id=1, source_target_pairs={{16,0},{32,16},{48,32},{64,48},{80,64},{96,80},{112,96},{128,112},... | collective-permute-start | bytes 196616 | tf_op jit(solution)/shard_map/ppermute | solution.py:84
  5.3 1.2 %slice.29 = s32[1,1]{1,0:T(1,128)} slice(s32[1,33]{1,0:T(1,128)} %param.8), slice={[0:1], [32:33]} | slice | bytes 8 | tf_op jit(solution)/shard_map/slice | solution.py:110
  6.6 0.7 slice.24
  7.3 0.0 copy-start.1
  7.3 0.7 gather_fusion
  8.0 1.4 %fusion.10 = (s32[32]{0:T(128)}, s32[32]{0:T(128)}) fusion(s32[1,33]{1,0:T(1,128)} %param.8, s32[32]{0:T(128)S(1)} %gather_fusion), kind=kLoop, calls=%fused_computation.30 | loop fusion | flops 96 | bytes 640 | tf_op jit(solution)/shard_map/jit(clip)/min | solution.py:55
  9.4 1.8 %compare_select_fusion.4.col_ref = s32[128]{0:T(128)} fusion(s32[128]{0:T(128)} %param.9, s32[]{:T(128)S(6)} %mul.6, s32[]{:T(128)} %bitcast.4), kind=kLoop, calls=%fused_computation.22 | loop fusion | flops 1792 | bytes 1032 | tf_op jit(solution)/shard_map/jit(_where)/select_n | solution.py:112
  11.2 0.7 compare_and_fusion
  12.0 0.0 collective-permute-done
  12.0 0.0 collective-permute-done.1
  12.0 1.6 %pad_maximum_fusion.ext_ref = f32[4,12288]{1,0:T(4,128)} fusion(f32[4,4096]{1,0:T(4,128)S(1)} %collective-permute-done.1, f32[4,4096]{1,0:T(4,128)} %param.6, f32[4,4096]{1,0:T(4,128)S(1)} %collective-permute-done), kind=kLoop, calls=%fused_computation.4 | loop fusion | flops 98304 | bytes 393216 | tf_op jit(solution)/shard_map/concatenate | solution.py:80
  13.5 0.0 copy-done.1
  13.5 8.6 %shard_map.64 = f32[4,4096]{1,0:T(4,128)} custom-call(s32[8]{0:T(128)} %copy-done.1, s32[32]{0:T(128)} %get-tuple-element.8.off_ref, s32[32]{0:T(128)} %get-tuple-element.7.cnt_ref, s32[128]{0:T(128)} %compare_select_fusion.4.col_ref, f32[4,12288]{1,0:T(4,128)} %pad_maximum_fusion.ext_ref, f32[128,128,128]{2,1,0:T(8,128)} %blk_ref.3), custom_call_target="tpu_custom_call" | custom-call | flops 16777216 | bytes 8585216 | tf_op jit(solution)/shard_map/pallas_call | solution.py:67
  22.1 7.5 %all-to-all-start = ((f32[4,16,256]{2,0,1:T(4,128)}), f32[4,16,256]{2,0,1:T(4,128)S(1)}, u32[]{:S(2)}, u32[]{:S(2)}) async-start(f32[4,16,256]{2,0,1:T(4,128)} %bitcast.25), calls=%async_computation | async-start | bytes 131072 | tf_op jit(solution)/shard_map/all_to_all | solution.py:120
  29.6 0.0 copy-done
  29.6 0.6 gather_fusion.1
  30.1 5.7 %all-to-all-done = f32[4,16,256]{2,0,1:T(4,128)S(1)} async-done(((f32[4,16,256]{2,0,1:T(4,128)}), f32[4,16,256]{2,0,1:T(4,128)S(1)}, u32[]{:S(2)}, u32[]{:S(2)}) %all-to-all-start) | async-done | bytes 65568 | tf_op jit(solution)/shard_map/all_to_all | solution.py:120
  35.9 0.4 convolution_bitcast_fusion.1
  36.3 0.1 copy.12
  36.4 0.1 all_to_all.55
  36.4 10.8 %all_to_all.70 = f32[16,4,256]{2,1,0:T(4,128)S(1)} all-to-all(f32[16,4,256]{2,1,0:T(4,128)S(1)} %all_to_all.55), channel_id=1, replica_groups=mesh['cells'=16,'tracer'=16] {'tracer'}, dimensions={0} | all-to-all | bytes 131072 | tf_op jit(solution)/shard_map/all_to_all | solution.py:122
  47.2 0.0 collective-permute-start.3
  47.2 0.5 collective-permute-start.2
  47.8 1.4 %collective-permute-done.3 = f32[4,4096]{1,0:T(4,128)S(1)} collective-permute-done((f32[4,4096]{1,0:T(4,128)S(1)}, f32[4,4096]{1,0:T(4,128)S(1)}, u32[]{:S(2)}, u32[]{:S(2)}) %collective-permute-start.3) | collective-permute-done | bytes 65568 | tf_op jit(solution)/shard_map/ppermute | solution.py:84
  49.2 3.0 %collective-permute-done.2 = f32[4,4096]{1,0:T(4,128)S(1)} collective-permute-done((f32[4,4096]{1,0:T(4,128)S(1)}, f32[4,4096]{1,0:T(4,128)S(1)}, u32[]{:S(2)}, u32[]{:S(2)}) %collective-permute-start.2) | collective-permute-done | bytes 65568 | tf_op jit(solution)/shard_map/ppermute | solution.py:82
  52.1 0.7 pad_maximum_fusion.1.ext_ref
  52.9 8.6 %shard_map.65 = f32[4,4096]{1,0:T(4,128)} custom-call(s32[8]{0:T(128)} %copy-done.1, s32[32]{0:T(128)} %get-tuple-element.8.off_ref, s32[32]{0:T(128)} %get-tuple-element.7.cnt_ref, s32[128]{0:T(128)} %compare_select_fusion.4.col_ref, f32[4,12288]{1,0:T(4,128)} %pad_maximum_fusion.1.ext_ref, f32[128,128,128]{2,1,0:T(8,128)} %blk_ref.3), custom_call_target="tpu_custom_call" | custom-call | flops 16777216 | bytes 8585216 | tf_op jit(solution)/shard_map/pallas_call | solution.py:67
  61.4 11.1 %all_to_all.71 = f32[4,16,256]{2,0,1:T(4,128)S(1)} all-to-all(f32[4,16,256]{2,0,1:T(4,128)} %bitcast.26), channel_id=1, replica_groups=mesh['cells'=16,'tracer'=16] {'tracer'}, dimensions={1} | all-to-all | bytes 131072 | tf_op jit(solution)/shard_map/all_to_all | solution.py:120
  72.6 0.4 convolution_bitcast_fusion
  73.0 0.1 copy.16
  73.0 0.1 all_to_all.62
  73.1 10.8 %all_to_all.72 = f32[16,4,256]{2,1,0:T(4,128)S(1)} all-to-all(f32[16,4,256]{2,1,0:T(4,128)S(1)} %all_to_all.62), channel_id=1, replica_groups=mesh['cells'=16,'tracer'=16] {'tracer'}, dimensions={0} | all-to-all | bytes 131072 | tf_op jit(solution)/shard_map/all_to_all | solution.py:122
  83.9 0.6 copy.24
  (6 shorter events, 0.1 us)
Async XLA Ops:
  0.0 29.6 %copy-start = (f32[8,64,64]{2,1,0:T(8,128)S(1)}, f32[8,64,64]{2,1,0:T(8,128)}, u32[]{:S(2)}) copy-start(f32[8,64,64]{2,1,0:T(8,128)} %param.11) | copy-start | bytes 393220
  0.0 11.9 %collective-permute-start = (f32[4,4096]{1,0:T(4,128)}, f32[4,4096]{1,0:T(4,128)S(1)}, u32[]{:S(2)}, u32[]{:S(2)}) collective-permute-start(f32[4,4096]{1,0:T(4,128)} %param.6), channel_id=1, source_target_pairs={{0,16},{16,32},{32,48},{48,64},{64,80},{80,96},{96,112},{112,128},... | collective-permute-start | bytes 196616 | tf_op jit(solution)/shard_map/ppermute | solution.py:82
  0.0 11.9 %collective-permute-start.1 = (f32[4,4096]{1,0:T(4,128)}, f32[4,4096]{1,0:T(4,128)S(1)}, u32[]{:S(2)}, u32[]{:S(2)}) collective-permute-start(f32[4,4096]{1,0:T(4,128)} %param.6), channel_id=1, source_target_pairs={{16,0},{32,16},{48,32},{64,48},{80,64},{96,80},{112,96},{128,112},... | collective-permute-start | bytes 196616 | tf_op jit(solution)/shard_map/ppermute | solution.py:84
  7.3 6.2 %copy-start.1 = (s32[8]{0:T(128)}, s32[8]{0:T(128)S(1)}, u32[]{:S(2)}) copy-start(s32[8]{0:T(128)S(1)} %broadcast_minimum_fusion.start_ref) | copy-start | bytes 100
  22.1 13.8 %all-to-all-start = ((f32[4,16,256]{2,0,1:T(4,128)}), f32[4,16,256]{2,0,1:T(4,128)S(1)}, u32[]{:S(2)}, u32[]{:S(2)}) async-start(f32[4,16,256]{2,0,1:T(4,128)} %bitcast.25), calls=%async_computation | async-start | bytes 131072 | tf_op jit(solution)/shard_map/all_to_all | solution.py:120
  47.2 1.9 %collective-permute-start.3 = (f32[4,4096]{1,0:T(4,128)S(1)}, f32[4,4096]{1,0:T(4,128)S(1)}, u32[]{:S(2)}, u32[]{:S(2)}) collective-permute-start(f32[4,4096]{1,0:T(4,128)S(1)} %bitcast.30), channel_id=1, source_target_pairs={{16,0},{32,16},{48,32},{64,48},{80,64},{96,80},{112,96},{128,112},... | collective-permute-start | bytes 196616 | tf_op jit(solution)/shard_map/ppermute | solution.py:84
  47.2 4.9 %collective-permute-start.2 = (f32[4,4096]{1,0:T(4,128)S(1)}, f32[4,4096]{1,0:T(4,128)S(1)}, u32[]{:S(2)}, u32[]{:S(2)}) collective-permute-start(f32[4,4096]{1,0:T(4,128)S(1)} %bitcast.31), channel_id=1, source_target_pairs={{0,16},{16,32},{32,48},{48,64},{64,80},{80,96},{96,112},{112,128},... | collective-permute-start | bytes 196616 | tf_op jit(solution)/shard_map/ppermute | solution.py:82

commit v3 on v2

v3 whole, which is shorter than its diff:
```python
import jax
import jax.numpy as jnp
from jax import lax
from jax.experimental import pallas as pl
from jax.experimental.pallas import tpu as pltpu
from jax.sharding import PartitionSpec as P

BLOCK = 128
STEPS = 2
ROWS_PER_STEP = 4
KMAX = 4


def transport_kernel(rp_ref, col_ref, left_ref, mid_ref, right_ref, blk_ref, out_ref, acc_ref):
    g = pl.program_id(0)
    spec, cells = mid_ref.shape
    nb_dev = cells // BLOCK
    nb_total = nb_dev * lax.axis_size("cells")
    first = (lax.axis_index("cells") - 1) * nb_dev
    window = blk_ref.shape[0]
    slots = col_ref.shape[0]
    base = jnp.minimum(rp_ref[g * ROWS_PER_STEP], slots - window)
    for rr in range(ROWS_PER_STEP):
        r = g * ROWS_PER_STEP + rr
        start = rp_ref[r]
        cnt = rp_ref[r + 1] - start
        off = start - base
        xs = []
        for k in range(KMAX):
            local = jnp.clip(off + k, 0, window - 1)
            col = lax.rem(col_ref[base + local] - first + 2 * nb_total, nb_total)
            col = jnp.clip(col, 0, 3 * nb_dev - 1)
            piece = col // nb_dev
            lane = pl.multiple_of((col - piece * nb_dev) * BLOCK, BLOCK)
            x = jnp.where(
                piece == 0,
                left_ref[:, pl.ds(lane, BLOCK)],
                jnp.where(piece == 1, mid_ref[:, pl.ds(lane, BLOCK)], right_ref[:, pl.ds(lane, BLOCK)]),
            )
            x = jnp.where(k < cnt, x, jnp.zeros_like(x))
            xs.append((local, x))
        for ic in range(BLOCK // 32):
            rows = slice(ic * 32, (ic + 1) * 32)
            accs = [None] * spec
            for local, x in xs:
                b = blk_ref[local, rows, :]
                for q in range(spec):
                    term = b * x[q:q + 1, :]
                    accs[q] = term if accs[q] is None else accs[q] + term
            for q in range(spec):
                acc_ref[q, rows, :] = accs[q]
        for q in range(spec):
            y = jnp.sum(acc_ref[q].T, axis=0, keepdims=True)
            out_ref[q:q + 1, rr * BLOCK:(rr + 1) * BLOCK] = y


def transport(left, mid, right, blocks, row_ptr, col_idx):
    spec, cells = mid.shape
    slots = blocks.shape[0]
    nrows = row_ptr.shape[0] - 1
    groups = nrows // ROWS_PER_STEP
    window = ROWS_PER_STEP * KMAX
    whole = lambda g, rp, ci: (0, 0)
    grid_spec = pltpu.PrefetchScalarGridSpec(
        num_scalar_prefetch=2,
        grid=(groups,),
        in_specs=[
            pl.BlockSpec(mid.shape, whole),
            pl.BlockSpec(mid.shape, whole),
            pl.BlockSpec(mid.shape, whole),
            pl.BlockSpec(
                (pl.Element(window), pl.Element(BLOCK), pl.Element(BLOCK)),
                lambda g, rp, ci: (jnp.minimum(rp[g * ROWS_PER_STEP], slots - window), 0, 0),
            ),
        ],
        out_specs=pl.BlockSpec((spec, ROWS_PER_STEP * BLOCK), lambda g, rp, ci: (0, g)),
        scratch_shapes=[pltpu.VMEM((spec, BLOCK, BLOCK), jnp.float32)],
    )
    flops = 2 * slots * BLOCK * BLOCK * spec
    return pl.pallas_call(
        transport_kernel,
        grid_spec=grid_spec,
        out_shape=jax.ShapeDtypeStruct((spec, nrows * BLOCK), jnp.float32),
        cost_estimate=pl.CostEstimate(
            flops=flops, bytes_accessed=blocks.size * 4 + 4 * mid.size * 4, transcendentals=0
        ),
    )(row_ptr, col_idx, left, mid, right, blocks)


def chemistry_local(moved, block_jac):
    spec, cells = moved.shape
    nblk = cells // BLOCK
    per_block = moved.reshape(spec, nblk, BLOCK)
    out = jnp.einsum("but,ubc->tbc", block_jac, per_block, precision=lax.Precision.HIGHEST)
    return out.reshape(spec, cells)


def halo(field):
    count = lax.axis_size("cells")
    left = lax.ppermute(field, "cells", [(i, (i + 1) % count) for i in range(count)])
    right = lax.ppermute(field, "cells", [((i + 1) % count, i) for i in range(count)])
    return left, right


def body(adjoint, blocks, row_ptr, col_idx, regime, jac):
    spec_dev, cells_dev = adjoint.shape
    nb_dev = cells_dev // BLOCK
    tracer_devices = lax.axis_size("tracer")
    tracer_index = lax.axis_index("tracer")
    pointers = row_ptr.reshape(-1)
    own_blocks = nb_dev // tracer_devices
    own_regime = lax.dynamic_slice_in_dim(regime, tracer_index * own_blocks, own_blocks)
    block_jac = jnp.take(jac, own_regime, axis=0)
    adjoint_field = adjoint
    for hour_step in range(STEPS):
        left, right = halo(adjoint_field)
        moved = transport(left, adjoint_field, right, blocks, pointers, col_idx)
        split = lax.all_to_all(moved, "tracer", 1, 0, tiled=True)
        reacted = chemistry_local(split, block_jac)
        adjoint_field = lax.all_to_all(reacted, "tracer", 0, 1, tiled=True)
    return adjoint_field


def solution(mesh):
    return jax.shard_map(
        body,
        mesh=mesh,
        in_specs=(
            P("tracer", "cells"),
            P("cells", None, None),
            P("cells", None),
            P("cells"),
            P("cells"),
            P(),
        ),
        out_specs=P("tracer", "cells"),
        check_vma=False,
    )
```

time: 85.3 us -> 80.3 us (0.941)
  other arithmetic: 6.22 us -> 0.74 us
  waiting for transfers between devices: 10.1 us -> 11.7 us
  local copies, waits for them, and re-layouts: 4.2 us -> 2.79 us
    concatenate x2 -> x0, other arithmetic: 2.27 us -> none  [with_halo(): jnp.concatenate([lax.ppermute(tail, axis, [(i, (i + 1) % count) for i in...]
    slice x2 -> x0, local copies, waits for them, and re-layouts: 1.98 us -> none  [the longest x1 1.24 us: body(): live_slot = slot_ids < pointers[-1]]
    select_n x2 -> x0, other arithmetic: 1.84 us -> none  [the longest x1 1.83 us: body(): local_col = jnp.where(live_slot, local_col, 0)]
    ppermute x4, waiting for transfers between devices: 4.4 us -> 5.99 us  [the longest x2 4.4 us: halo(): lax.ppermute(field, 'cells', [(i, (i + 1) % count) for i in range(count)])]
    min x2 -> x0, other arithmetic: 1.36 us -> none  [the longest x1 1.36 us: transport(): cnts = jnp.clip(row_ptr[1:] - row_ptr[:-1], 0, KMAX).astype(jnp.int32)]
    unnamed x5 -> x13, local copies, waits for them, and re-layouts: 0.64 us -> 1.9 us
  transfers between devices with their start and end apart: 5 -> 5, of which waited for: 3 -> 5; matrix products, arithmetic and copies ran while one was open for 8% -> 2% of each run, Pallas kernels for 0% -> 0%
where the time goes in v3:
time: 80.3 us; the launch traced here: 79.6 us
  blocking collectives  32.9 us (41%)
  Pallas kernels  17.4 us (22%)
  starting transfers between devices  13.3 us (17%)
  waiting for transfers between devices  11.7 us (15%)
  local copies, waits for them, and re-layouts  2.79 us (3%)
    all_to_all x2, blocking collectives, body(): adjoint_field = lax.all_to_all(reacted, 'tracer', 0, 1, tiled=True)  21.6 us
    pallas_call x2, Pallas kernels, transport(): pl.pallas_call(transport_kernel, grid_spec=grid_spec, out_shape=jax.Shape...  17.4 us
    all_to_all x1, blocking collectives, body(): split = lax.all_to_all(moved, 'tracer', 1, 0, tiled=True)  11.3 us
    all_to_all x1, starting transfers between devices, body(): split = lax.all_to_all(moved, 'tracer', 1, 0, tiled=True)  7.48 us
    all_to_all x1, waiting for transfers between devices, body(): split = lax.all_to_all(moved, 'tracer', 1, 0, tiled=True)  5.73 us
    ppermute x2, starting transfers between devices, halo(): lax.ppermute(field, 'cells', [((i + 1) % count, i) for i in range(count)])  5.42 us
    ppermute x2, waiting for transfers between devices, halo(): lax.ppermute(field, 'cells', [(i, (i + 1) % count) for i in range(count)])  4.4 us
    unnamed x13, local copies, waits for them, and re-layouts  1.9 us
  transfers between devices with their start and end apart: 5, of which 5 were waited for; matrix products, arithmetic and copies ran while one was open for 2% of the time, Pallas kernels for 0%

profile of v3, /device:TPU:2, one launch (start us, length us, event | category | flops | bytes accessed | tf_op | source)
XLA Modules:
  0.0 79.6 jit_solution(10275775588042960031)
XLA Ops:
  0.0 0.0 copy-start
  0.0 0.0 collective-permute-start
  0.0 5.3 %collective-permute-start.1 = (f32[4,4096]{1,0:T(4,128)}, f32[4,4096]{1,0:T(4,128)S(1)}, u32[]{:S(2)}, u32[]{:S(2)}) collective-permute-start(f32[4,4096]{1,0:T(4,128)} %mid_ref.1), channel_id=1, source_target_pairs={{16,0},{32,16},{48,32},{64,48},{80,64},{96,80},{112,96},{128,112},... | collective-permute-start | bytes 196616 | tf_op jit(solution)/shard_map/ppermute | solution.py:101
  5.3 0.7 compare_and_fusion
  6.1 1.4 %collective-permute-done.left_ref = f32[4,4096]{1,0:T(4,128)S(1)} collective-permute-done((f32[4,4096]{1,0:T(4,128)}, f32[4,4096]{1,0:T(4,128)S(1)}, u32[]{:S(2)}, u32[]{:S(2)}) %collective-permute-start) | collective-permute-done | bytes 65568 | tf_op jit(solution)/shard_map/ppermute | solution.py:100
  7.5 0.0 copy-start.2
  7.5 0.1 collective-permute-done.1.right_ref
  7.5 0.0 copy-start.3
  7.5 0.5 copy-done.2
  8.1 0.1 copy-done.3
  8.2 8.7 %shard_map.64 = f32[4,4096]{1,0:T(4,128)} custom-call(s32[33]{0:T(128)} %bitcast.23, s32[128]{0:T(128)} %col_ref.3, f32[4,4096]{1,0:T(4,128)} %copy-done.2, f32[4,4096]{1,0:T(4,128)} %mid_ref.1, f32[4,4096]{1,0:T(4,128)} %copy-done.3, f32[128,128,128]{2,1,0:T(8,128)} %blk_ref.3), custom_call_target="tpu_custom_call" | custom-call | flops 16777216 | bytes 8650752 | tf_op jit(solution)/shard_map/pallas_call | solution.py:80
  16.8 7.5 %all-to-all-start = ((f32[4,16,256]{2,0,1:T(4,128)}), f32[4,16,256]{2,0,1:T(4,128)S(1)}, u32[]{:S(2)}, u32[]{:S(2)}) async-start(f32[4,16,256]{2,0,1:T(4,128)} %bitcast.18), calls=%async_computation | async-start | bytes 131072 | tf_op jit(solution)/shard_map/all_to_all | solution.py:118
  24.3 0.0 copy-done
  24.3 0.6 gather_fusion
  24.9 5.7 %all-to-all-done = f32[4,16,256]{2,0,1:T(4,128)S(1)} async-done(((f32[4,16,256]{2,0,1:T(4,128)}), f32[4,16,256]{2,0,1:T(4,128)S(1)}, u32[]{:S(2)}, u32[]{:S(2)}) %all-to-all-start) | async-done | bytes 65568 | tf_op jit(solution)/shard_map/all_to_all | solution.py:118
  30.7 0.4 convolution_bitcast_fusion.1
  31.1 0.1 copy.12
  31.1 0.1 all_to_all.55
  31.2 10.8 %all_to_all.70 = f32[16,4,256]{2,1,0:T(4,128)S(1)} all-to-all(f32[16,4,256]{2,1,0:T(4,128)S(1)} %all_to_all.55), channel_id=1, replica_groups=mesh['cells'=16,'tracer'=16] {'tracer'}, dimensions={0} | all-to-all | bytes 131072 | tf_op jit(solution)/shard_map/all_to_all | solution.py:120
  42.0 0.0 copy-start.1
  42.0 0.1 collective-permute-start.3
  42.1 0.4 collective-permute-start.2
  42.5 1.5 %collective-permute-done.3.right_ref = f32[4,4096]{1,0:T(4,128)S(1)} collective-permute-done((f32[4,4096]{1,0:T(4,128)S(1)}, f32[4,4096]{1,0:T(4,128)S(1)}, u32[]{:S(2)}, u32[]{:S(2)}) %collective-permute-start.3) | collective-permute-done | bytes 65568 | tf_op jit(solution)/shard_map/ppermute | solution.py:101
  44.0 0.0 copy-start.4
  44.0 3.0 %collective-permute-done.2.left_ref = f32[4,4096]{1,0:T(4,128)S(1)} collective-permute-done((f32[4,4096]{1,0:T(4,128)S(1)}, f32[4,4096]{1,0:T(4,128)S(1)}, u32[]{:S(2)}, u32[]{:S(2)}) %collective-permute-start.2) | collective-permute-done | bytes 65568 | tf_op jit(solution)/shard_map/ppermute | solution.py:100
  47.0 0.0 copy-done.1
  47.0 0.0 copy-done.4
  47.0 0.0 copy-start.5
  47.0 0.6 copy-done.5
  47.7 8.7 %shard_map.65 = f32[4,4096]{1,0:T(4,128)} custom-call(s32[33]{0:T(128)} %bitcast.24, s32[128]{0:T(128)} %col_ref.3, f32[4,4096]{1,0:T(4,128)} %copy-done.5, f32[4,4096]{1,0:T(4,128)} %bitcast.17, f32[4,4096]{1,0:T(4,128)} %copy-done.4, f32[128,128,128]{2,1,0:T(8,128)} %blk_ref.3), custom_call_target="tpu_custom_call" | custom-call | flops 16777216 | bytes 8650752 | tf_op jit(solution)/shard_map/pallas_call | solution.py:80
  56.3 11.3 %all_to_all.71 = f32[4,16,256]{2,0,1:T(4,128)S(1)} all-to-all(f32[4,16,256]{2,0,1:T(4,128)} %bitcast.19), channel_id=1, replica_groups=mesh['cells'=16,'tracer'=16] {'tracer'}, dimensions={1} | all-to-all | bytes 131072 | tf_op jit(solution)/shard_map/all_to_all | solution.py:118
  67.7 0.4 convolution_bitcast_fusion
  68.1 0.1 copy.16
  68.1 0.1 all_to_all.62
  68.2 10.8 %all_to_all.72 = f32[16,4,256]{2,1,0:T(4,128)S(1)} all-to-all(f32[16,4,256]{2,1,0:T(4,128)S(1)} %all_to_all.62), channel_id=1, replica_groups=mesh['cells'=16,'tracer'=16] {'tracer'}, dimensions={0} | all-to-all | bytes 131072 | tf_op jit(solution)/shard_map/all_to_all | solution.py:120
  79.0 0.6 copy.24
  (3 shorter events, 0.1 us)
Async XLA Ops:
  0.0 24.3 %copy-start = (f32[8,64,64]{2,1,0:T(8,128)S(1)}, f32[8,64,64]{2,1,0:T(8,128)}, u32[]{:S(2)}) copy-start(f32[8,64,64]{2,1,0:T(8,128)} %param.11) | copy-start | bytes 393220
  0.0 7.5 %collective-permute-start = (f32[4,4096]{1,0:T(4,128)}, f32[4,4096]{1,0:T(4,128)S(1)}, u32[]{:S(2)}, u32[]{:S(2)}) collective-permute-start(f32[4,4096]{1,0:T(4,128)} %mid_ref.1), channel_id=1, source_target_pairs={{0,16},{16,32},{32,48},{48,64},{64,80},{80,96},{96,112},{112,128},... | collective-permute-start | bytes 196616 | tf_op jit(solution)/shard_map/ppermute | solution.py:100
  0.0 7.5 %collective-permute-start.1 = (f32[4,4096]{1,0:T(4,128)}, f32[4,4096]{1,0:T(4,128)S(1)}, u32[]{:S(2)}, u32[]{:S(2)}) collective-permute-start(f32[4,4096]{1,0:T(4,128)} %mid_ref.1), channel_id=1, source_target_pairs={{16,0},{32,16},{48,32},{64,48},{80,64},{96,80},{112,96},{128,112},... | collective-permute-start | bytes 196616 | tf_op jit(solution)/shard_map/ppermute | solution.py:101
  7.5 0.6 copy-start.2
  7.5 0.6 copy-start.3
  16.8 13.8 %all-to-all-start = ((f32[4,16,256]{2,0,1:T(4,128)}), f32[4,16,256]{2,0,1:T(4,128)S(1)}, u32[]{:S(2)}, u32[]{:S(2)}) async-start(f32[4,16,256]{2,0,1:T(4,128)} %bitcast.18), calls=%async_computation | async-start | bytes 131072 | tf_op jit(solution)/shard_map/all_to_all | solution.py:118
  42.0 5.0 %copy-start.1 = (f32[16,4,256]{2,1,0:T(4,128)}, f32[16,4,256]{2,1,0:T(4,128)S(1)}, u32[]{:S(2)}) copy-start(f32[16,4,256]{2,1,0:T(4,128)S(1)} %all_to_all.70) | copy-start | bytes 196612
  42.0 2.0 %collective-permute-start.3 = (f32[4,4096]{1,0:T(4,128)S(1)}, f32[4,4096]{1,0:T(4,128)S(1)}, u32[]{:S(2)}, u32[]{:S(2)}) collective-permute-start(f32[4,4096]{1,0:T(4,128)S(1)} %bitcast.15), channel_id=1, source_target_pairs={{16,0},{32,16},{48,32},{64,48},{80,64},{96,80},{112,96},{128,112},... | collective-permute-start | bytes 196616 | tf_op jit(solution)/shard_map/ppermute | solution.py:101
  42.1 4.9 %collective-permute-start.2 = (f32[4,4096]{1,0:T(4,128)S(1)}, f32[4,4096]{1,0:T(4,128)S(1)}, u32[]{:S(2)}, u32[]{:S(2)}) collective-permute-start(f32[4,4096]{1,0:T(4,128)S(1)} %bitcast.16), channel_id=1, source_target_pairs={{0,16},{16,32},{32,48},{48,64},{64,80},{80,96},{96,112},{112,128},... | collective-permute-start | bytes 196616 | tf_op jit(solution)/shard_map/ppermute | solution.py:100
  44.0 3.0 %copy-start.4 = (f32[4,4096]{1,0:T(4,128)}, f32[4,4096]{1,0:T(4,128)S(1)}, u32[]{:S(2)}) copy-start(f32[4,4096]{1,0:T(4,128)S(1)} %collective-permute-done.3.right_ref) | copy-start | bytes 196612
  47.0 0.6 copy-start.5

commit v4 on v3

--- a/solution.py
+++ b/solution.py
@@ -87,12 +87,19 @@
     )(row_ptr, col_idx, left, mid, right, blocks)
 
 
-def chemistry_local(moved, block_jac):
-    spec, cells = moved.shape
+def chemistry_own(moved_all, block_jac):
+    spec, cells = moved_all.shape
     nblk = cells // BLOCK
-    per_block = moved.reshape(spec, nblk, BLOCK)
+    per_block = moved_all.reshape(spec, nblk, BLOCK)
     out = jnp.einsum("but,ubc->tbc", block_jac, per_block, precision=lax.Precision.HIGHEST)
-    return out.reshape(spec, cells)
+    return out.reshape(out.shape[0], cells)
+
+
+def gather_species(moved):
+    peers = lax.axis_size("tracer")
+    copies = jnp.broadcast_to(moved[None], (peers,) + moved.shape)
+    every = lax.all_to_all(copies, "tracer", 0, 0, tiled=True)
+    return every.reshape(peers * moved.shape[0], moved.shape[1])
 
 
 def halo(field):
@@ -105,19 +112,15 @@
 def body(adjoint, blocks, row_ptr, col_idx, regime, jac):
     spec_dev, cells_dev = adjoint.shape
     nb_dev = cells_dev // BLOCK
-    tracer_devices = lax.axis_size("tracer")
     tracer_index = lax.axis_index("tracer")
     pointers = row_ptr.reshape(-1)
-    own_blocks = nb_dev // tracer_devices
-    own_regime = lax.dynamic_slice_in_dim(regime, tracer_index * own_blocks, own_blocks)
-    block_jac = jnp.take(jac, own_regime, axis=0)
+    own_jac = lax.dynamic_slice_in_dim(jac, tracer_index * spec_dev, spec_dev, 2)
+    block_jac = jnp.take(own_jac, regime, axis=0)
     adjoint_field = adjoint
     for hour_step in range(STEPS):
         left, right = halo(adjoint_field)
         moved = transport(left, adjoint_field, right, blocks, pointers, col_idx)
-        split = lax.all_to_all(moved, "tracer", 1, 0, tiled=True)
-        reacted = chemistry_local(split, block_jac)
-        adjoint_field = lax.all_to_all(reacted, "tracer", 0, 1, tiled=True)
+        adjoint_field = chemistry_own(gather_species(moved), block_jac)
     return adjoint_field
 
 

time: 80.3 us -> 86.8 us (1.081)
  blocking collectives: 32.9 us -> 18.9 us
  waiting for transfers between devices: 11.7 us -> 21 us
  matrix products: 0.75 us -> 5.12 us
  local copies, waits for them, and re-layouts: 2.79 us -> 6.51 us
  starting transfers between devices: 13.3 us -> 16.9 us
    all_to_all x3 -> x1, blocking collectives: 32.9 us -> 18.9 us  [gather_species(): every = lax.all_to_all(copies, 'tracer', 0, 0, tiled=True)]
    all_to_all x1, waiting for transfers between devices: 5.73 us -> 13.9 us  [gather_species(): every = lax.all_to_all(copies, 'tracer', 0, 0, tiled=True)]
    dot_general x2, matrix products: 0.75 us -> 5.12 us  [chemistry_own(): jnp.einsum('but,ubc->tbc', block_jac, per_block, precision=lax.Precision....]
    ppermute x2, starting transfers between devices: 5.42 us -> 9.45 us  [halo(): lax.ppermute(field, 'cells', [((i + 1) % count, i) for i in range(count)])]
    broadcast_in_dim x0 -> x2, local copies, waits for them, and re-layouts: none -> 3.05 us  [gather_species(): copies = jnp.broadcast_to(moved[None], (peers,) + moved.shape)]
    another operation x0 -> x2, local copies, waits for them, and re-layouts: none -> 1.44 us  [chemistry_own(): per_block = moved_all.reshape(spec, nblk, BLOCK)]
    unnamed x13 -> x14, local copies, waits for them, and re-layouts: 1.9 us -> 1.28 us
  transfers between devices with their start and end apart: 5 -> 5, of which waited for: 5 -> 5; matrix products, arithmetic and copies ran while one was open for 2% -> 1% of each run, Pallas kernels for 0% -> 0%
where the time goes in v4:
time: 86.8 us; the launch traced here: 86 us
  waiting for transfers between devices  21 us (24%)
  blocking collectives  18.9 us (22%)
  Pallas kernels  17.3 us (20%)
  starting transfers between devices  16.9 us (19%)
  local copies, waits for them, and re-layouts  6.51 us (8%)
  matrix products  5.12 us (6%)
    all_to_all x1, blocking collectives, gather_species(): every = lax.all_to_all(copies, 'tracer', 0, 0, tiled=True)  18.9 us
    pallas_call x2, Pallas kernels, transport(): pl.pallas_call(transport_kernel, grid_spec=grid_spec, out_shape=jax.Shape...  17.3 us
    all_to_all x1, waiting for transfers between devices, gather_species(): every = lax.all_to_all(copies, 'tracer', 0, 0, tiled=True)  13.9 us
    ppermute x2, starting transfers between devices, halo(): lax.ppermute(field, 'cells', [((i + 1) % count, i) for i in range(count)])  9.45 us
    all_to_all x1, starting transfers between devices, gather_species(): every = lax.all_to_all(copies, 'tracer', 0, 0, tiled=True)  7.48 us
    ppermute x2, waiting for transfers between devices, halo(): lax.ppermute(field, 'cells', [(i, (i + 1) % count) for i in range(count)])  5.13 us
    dot_general x2, matrix products, chemistry_own(): jnp.einsum('but,ubc->tbc', block_jac, per_block, precision=lax.Precision....  5.12 us
    broadcast_in_dim x2, local copies, waits for them, and re-layouts, gather_species(): copies = jnp.broadcast_to(moved[None], (peers,) + moved.shape)  3.05 us
  transfers between devices with their start and end apart: 5, of which 5 were waited for; matrix products, arithmetic and copies ran while one was open for 1% of the time, Pallas kernels for 0%

profile of v4, /device:TPU:2, one launch (start us, length us, event | category | flops | bytes accessed | tf_op | source)
XLA Modules:
  0.0 86.0 jit_solution(5945149241488369704)
XLA Ops:
  0.0 0.0 copy-start
  0.0 0.0 copy-start.6
  0.0 0.0 collective-permute-start
  0.0 5.3 %collective-permute-start.1 = (f32[4,4096]{1,0:T(4,128)}, f32[4,4096]{1,0:T(4,128)S(1)}, u32[]{:S(2)}, u32[]{:S(2)}) collective-permute-start(f32[4,4096]{1,0:T(4,128)} %mid_ref.1), channel_id=1, source_target_pairs={{16,0},{32,16},{48,32},{64,48},{80,64},{96,80},{112,96},{128,112},... | collective-permute-start | bytes 196616 | tf_op jit(solution)/shard_map/ppermute | solution.py:108
  5.3 2.1 %collective-permute-done.left_ref = f32[4,4096]{1,0:T(4,128)S(1)} collective-permute-done((f32[4,4096]{1,0:T(4,128)}, f32[4,4096]{1,0:T(4,128)S(1)}, u32[]{:S(2)}, u32[]{:S(2)}) %collective-permute-start) | collective-permute-done | bytes 65568 | tf_op jit(solution)/shard_map/ppermute | solution.py:107
  7.5 0.0 copy-start.3
  7.5 0.1 collective-permute-done.1.right_ref
  7.5 0.0 copy-start.5
  7.5 0.5 copy-done.3
  8.1 0.1 copy-done.5
  8.2 8.7 %shard_map.64 = f32[4,4096]{1,0:T(4,128)} custom-call(s32[33]{0:T(128)} %bitcast.9, s32[128]{0:T(128)} %col_ref.3, f32[4,4096]{1,0:T(4,128)} %copy-done.3, f32[4,4096]{1,0:T(4,128)} %mid_ref.1, f32[4,4096]{1,0:T(4,128)} %copy-done.5, f32[128,128,128]{2,1,0:T(8,128)} %blk_ref.3), custom_call_target="tpu_custom_call" | custom-call | flops 16777216 | bytes 8650752 | tf_op jit(solution)/shard_map/pallas_call | solution.py:80
  16.8 2.0 %broadcast_in_dim.24 = f32[16,4,4096]{2,1,0:T(4,128)} broadcast(f32[4,4096]{1,0:T(4,128)} %shard_map.64), dimensions={1,2} | broadcast | bytes 1114112 | tf_op jit(solution)/shard_map/broadcast_in_dim | solution.py:100
  18.9 7.5 %all-to-all-start = ((f32[16,4,4096]{2,1,0:T(4,128)}), f32[16,4,4096]{2,1,0:T(4,128)S(1)}, u32[]{:S(2)}, u32[]{:S(2)}) async-start(f32[16,4,4096]{2,1,0:T(4,128)} %broadcast_in_dim.24), calls=%async_computation | async-start | bytes 2097152 | tf_op jit(solution)/shard_map/all_to_all | solution.py:101
  26.3 0.0 copy-done.6
  26.4 0.0 copy-done
  26.4 0.1 constant_dynamic-slice_fusion
  26.5 0.6 gather_fusion
  27.2 13.9 %all-to-all-done = f32[16,4,4096]{2,1,0:T(4,128)S(1)} async-done(((f32[16,4,4096]{2,1,0:T(4,128)}), f32[16,4,4096]{2,1,0:T(4,128)S(1)}, u32[]{:S(2)}, u32[]{:S(2)}) %all-to-all-start) | async-done | bytes 1048608 | tf_op jit(solution)/shard_map/all_to_all | solution.py:101
  41.1 0.7 reshape_reshape.6
  41.8 2.2 %convolution_bitcast_fusion.1.mid_ref = f32[4,4096]{1,0:T(4,128)S(1)} fusion(f32[64,32,128]{2,1,0:T(8,128)S(1)} %reshape_reshape.6, f32[32,64,4]{2,1,0:T(8,128)S(1)} %gather_fusion, pred[32]{0:T(512)(128)(4,1)S(1)} %compare_and_fusion), kind=kOutput, calls=%fused_computation.2 | convolution fusion | flops 12591104 | bytes 1146912 | tf_op jit(solution)/shard_map/but,ubc->tbc/dot_general | solution.py:94
  44.0 0.0 copy-start.1
  44.1 4.1 %collective-permute-start.3 = (f32[4,4096]{1,0:T(4,128)S(1)}, f32[4,4096]{1,0:T(4,128)S(1)}, u32[]{:S(2)}, u32[]{:S(2)}) collective-permute-start(f32[4,4096]{1,0:T(4,128)S(1)} %convolution_bitcast_fusion.1.mid_ref), channel_id=1, source_target_pairs={{16,0},{32,16},{48,32},{64,48},{80,64},{96,80},{112,96},{128,112},... | collective-permute-start | bytes 196616 | tf_op jit(solution)/shard_map/ppermute | solution.py:108
  48.2 0.0 collective-permute-start.2
  48.2 1.9 %collective-permute-done.3.right_ref = f32[4,4096]{1,0:T(4,128)S(1)} collective-permute-done((f32[4,4096]{1,0:T(4,128)S(1)}, f32[4,4096]{1,0:T(4,128)S(1)}, u32[]{:S(2)}, u32[]{:S(2)}) %collective-permute-start.3) | collective-permute-done | bytes 65568 | tf_op jit(solution)/shard_map/ppermute | solution.py:108
  50.1 0.0 copy-start.2
  50.1 3.0 %collective-permute-done.2.left_ref = f32[4,4096]{1,0:T(4,128)S(1)} collective-permute-done((f32[4,4096]{1,0:T(4,128)S(1)}, f32[4,4096]{1,0:T(4,128)S(1)}, u32[]{:S(2)}, u32[]{:S(2)}) %collective-permute-start.2) | collective-permute-done | bytes 65568 | tf_op jit(solution)/shard_map/ppermute | solution.py:107
  53.1 0.0 copy-done.1
  53.1 0.0 copy-done.2
  53.1 0.0 copy-start.4
  53.1 0.6 copy-done.4
  53.7 8.7 %shard_map.65 = f32[4,4096]{1,0:T(4,128)} custom-call(s32[33]{0:T(128)} %bitcast.10, s32[128]{0:T(128)} %col_ref.3, f32[4,4096]{1,0:T(4,128)} %copy-done.4, f32[4,4096]{1,0:T(4,128)} %copy-done.1, f32[4,4096]{1,0:T(4,128)} %copy-done.2, f32[128,128,128]{2,1,0:T(8,128)} %blk_ref.3), custom_call_target="tpu_custom_call" | custom-call | flops 16777216 | bytes 8650752 | tf_op jit(solution)/shard_map/pallas_call | solution.py:80
  62.4 1.0 %broadcast_in_dim.28 = f32[16,4,4096]{2,1,0:T(4,128)S(1)} broadcast(f32[4,4096]{1,0:T(4,128)} %shard_map.65), dimensions={1,2} | broadcast | bytes 1114112 | tf_op jit(solution)/shard_map/broadcast_in_dim | solution.py:100
  63.5 18.9 %all_to_all.10 = f32[16,4,4096]{2,1,0:T(4,128)S(1)} all-to-all(f32[16,4,4096]{2,1,0:T(4,128)S(1)} %broadcast_in_dim.28), channel_id=1, replica_groups=mesh['cells'=16,'tracer'=16] {'tracer'}, dimensions={0} | all-to-all | bytes 2097152 | tf_op jit(solution)/shard_map/all_to_all | solution.py:101
  82.4 0.7 reshape_reshape.7
  83.1 2.9 %convolution_bitcast_fusion = f32[4,4096]{1,0:T(4,128)} fusion(f32[64,32,128]{2,1,0:T(8,128)S(1)} %reshape_reshape.7, f32[32,64,4]{2,1,0:T(8,128)S(1)} %gather_fusion, pred[32]{0:T(512)(128)(4,1)S(1)} %compare_and_fusion), kind=kOutput, calls=%fused_computation.1 | convolution fusion | flops 12591104 | bytes 1146912 | tf_op jit(solution)/shard_map/but,ubc->tbc/dot_general | solution.py:94
  (3 shorter events, 0.0 us)
Async XLA Ops:
  0.0 26.4 %copy-start = (f32[8,64,64]{2,1,0:T(8,128)S(1)}, f32[8,64,64]{2,1,0:T(8,128)}, u32[]{:S(2)}) copy-start(f32[8,64,64]{2,1,0:T(8,128)} %param.11) | copy-start | bytes 393220
  0.0 26.3 %copy-start.6 = (s32[32]{0:T(128)S(1)}, s32[32]{0:T(128)}, u32[]{:S(2)}) copy-start(s32[32]{0:T(128)} %param.10) | copy-start | bytes 388
  0.0 7.5 %collective-permute-start = (f32[4,4096]{1,0:T(4,128)}, f32[4,4096]{1,0:T(4,128)S(1)}, u32[]{:S(2)}, u32[]{:S(2)}) collective-permute-start(f32[4,4096]{1,0:T(4,128)} %mid_ref.1), channel_id=1, source_target_pairs={{0,16},{16,32},{32,48},{48,64},{64,80},{80,96},{96,112},{112,128},... | collective-permute-start | bytes 196616 | tf_op jit(solution)/shard_map/ppermute | solution.py:107
  0.0 7.5 %collective-permute-start.1 = (f32[4,4096]{1,0:T(4,128)}, f32[4,4096]{1,0:T(4,128)S(1)}, u32[]{:S(2)}, u32[]{:S(2)}) collective-permute-start(f32[4,4096]{1,0:T(4,128)} %mid_ref.1), channel_id=1, source_target_pairs={{16,0},{32,16},{48,32},{64,48},{80,64},{96,80},{112,96},{128,112},... | collective-permute-start | bytes 196616 | tf_op jit(solution)/shard_map/ppermute | solution.py:108
  7.5 0.6 copy-start.3
  7.5 0.6 copy-start.5
  18.9 22.2 %all-to-all-start = ((f32[16,4,4096]{2,1,0:T(4,128)}), f32[16,4,4096]{2,1,0:T(4,128)S(1)}, u32[]{:S(2)}, u32[]{:S(2)}) async-start(f32[16,4,4096]{2,1,0:T(4,128)} %broadcast_in_dim.24), calls=%async_computation | async-start | bytes 2097152 | tf_op jit(solution)/shard_map/all_to_all | solution.py:101
  44.0 9.1 %copy-start.1 = (f32[4,4096]{1,0:T(4,128)}, f32[4,4096]{1,0:T(4,128)S(1)}, u32[]{:S(2)}) copy-start(f32[4,4096]{1,0:T(4,128)S(1)} %convolution_bitcast_fusion.1.mid_ref) | copy-start | bytes 196612
  44.1 6.1 %collective-permute-start.3 = (f32[4,4096]{1,0:T(4,128)S(1)}, f32[4,4096]{1,0:T(4,128)S(1)}, u32[]{:S(2)}, u32[]{:S(2)}) collective-permute-start(f32[4,4096]{1,0:T(4,128)S(1)} %convolution_bitcast_fusion.1.mid_ref), channel_id=1, source_target_pairs={{16,0},{32,16},{48,32},{64,48},{80,64},{96,80},{112,96},{128,112},... | collective-permute-start | bytes 196616 | tf_op jit(solution)/shard_map/ppermute | solution.py:108
  48.2 4.9 %collective-permute-start.2 = (f32[4,4096]{1,0:T(4,128)S(1)}, f32[4,4096]{1,0:T(4,128)S(1)}, u32[]{:S(2)}, u32[]{:S(2)}) collective-permute-start(f32[4,4096]{1,0:T(4,128)S(1)} %convolution_bitcast_fusion.1.mid_ref), channel_id=1, source_target_pairs={{0,16},{16,32},{32,48},{48,64},{64,80},{80,96},{96,112},{112,128},... | collective-permute-start | bytes 196616 | tf_op jit(solution)/shard_map/ppermute | solution.py:107
  50.1 3.0 %copy-start.2 = (f32[4,4096]{1,0:T(4,128)}, f32[4,4096]{1,0:T(4,128)S(1)}, u32[]{:S(2)}) copy-start(f32[4,4096]{1,0:T(4,128)S(1)} %collective-permute-done.3.right_ref) | copy-start | bytes 196612
  53.1 0.6 copy-start.4

commit v5 on v3

--- a/solution.py
+++ b/solution.py
@@ -115,6 +115,8 @@
     for hour_step in range(STEPS):
         left, right = halo(adjoint_field)
         moved = transport(left, adjoint_field, right, blocks, pointers, col_idx)
+        if hour_step == 0:
+            moved, block_jac = lax.optimization_barrier((moved, block_jac))
         split = lax.all_to_all(moved, "tracer", 1, 0, tiled=True)
         reacted = chemistry_local(split, block_jac)
         adjoint_field = lax.all_to_all(reacted, "tracer", 0, 1, tiled=True)

time: 80.3 us -> 80.1 us (level)
  blocking collectives: 32.9 us -> 46.7 us
  starting transfers between devices: 13.3 us -> 5.82 us
  waiting for transfers between devices: 11.7 us -> 5.33 us
    all_to_all x1 -> x2, blocking collectives: 11.3 us -> 25.1 us  [body(): split = lax.all_to_all(moved, 'tracer', 1, 0, tiled=True)]
    all_to_all x1 -> x0, starting transfers between devices: 7.48 us -> none  [body(): split = lax.all_to_all(moved, 'tracer', 1, 0, tiled=True)]
    all_to_all x1 -> x0, waiting for transfers between devices: 5.73 us -> none  [body(): split = lax.all_to_all(moved, 'tracer', 1, 0, tiled=True)]
  transfers between devices with their start and end apart: 5 -> 4, of which waited for: 5 -> 4; matrix products, arithmetic and copies ran while one was open for 2% -> 2% of each run, Pallas kernels for 0% -> 0%
where the time goes in v5:
time: 80.1 us; the launch traced here: 79.4 us
  blocking collectives  46.7 us (58%)
  Pallas kernels  17.3 us (22%)
  starting transfers between devices  5.82 us (7%)
  waiting for transfers between devices  5.33 us (7%)
  local copies, waits for them, and re-layouts  2.79 us (3%)
  other arithmetic  0.81 us (1%)
    all_to_all x2, blocking collectives, body(): split = lax.all_to_all(moved, 'tracer', 1, 0, tiled=True)  25.1 us
    all_to_all x2, blocking collectives, body(): adjoint_field = lax.all_to_all(reacted, 'tracer', 0, 1, tiled=True)  21.6 us
    pallas_call x2, Pallas kernels, transport(): pl.pallas_call(transport_kernel, grid_spec=grid_spec, out_shape=jax.Shape...  17.3 us
    ppermute x2, starting transfers between devices, halo(): lax.ppermute(field, 'cells', [((i + 1) % count, i) for i in range(count)])  5.42 us
    ppermute x2, waiting for transfers between devices, halo(): lax.ppermute(field, 'cells', [(i, (i + 1) % count) for i in range(count)])  3.75 us
    unnamed x13, local copies, waits for them, and re-layouts  1.9 us
  transfers between devices with their start and end apart: 4, of which 4 were waited for; matrix products, arithmetic and copies ran while one was open for 2% of the time, Pallas kernels for 0%

profile of v5, /device:TPU:2, one launch (start us, length us, event | category | flops | bytes accessed | tf_op | source)
XLA Modules:
  0.0 79.4 jit_solution(16275820193639169532)
XLA Ops:
  0.0 0.0 copy-start
  0.0 0.0 collective-permute-start
  0.0 5.3 %collective-permute-start.1 = (f32[4,4096]{1,0:T(4,128)}, f32[4,4096]{1,0:T(4,128)S(1)}, u32[]{:S(2)}, u32[]{:S(2)}) collective-permute-start(f32[4,4096]{1,0:T(4,128)} %mid_ref.1), channel_id=1, source_target_pairs={{16,0},{32,16},{48,32},{64,48},{80,64},{96,80},{112,96},{128,112},... | collective-permute-start | bytes 196616 | tf_op jit(solution)/shard_map/ppermute | solution.py:101
  5.3 0.7 compare_and_fusion
  6.1 0.0 copy-done
  6.1 0.6 gather_fusion
  6.6 0.1 broadcast_select_fusion
  6.7 0.8 collective-permute-done.left_ref
  7.5 0.0 copy-start.2
  7.5 0.1 collective-permute-done.1.right_ref
  7.5 0.0 copy-start.3
  7.5 0.5 copy-done.2
  8.1 0.1 copy-done.3
  8.2 8.7 %shard_map.64 = f32[4,4096]{1,0:T(4,128)} custom-call(s32[33]{0:T(128)} %bitcast.25, s32[128]{0:T(128)} %col_ref.3, f32[4,4096]{1,0:T(4,128)} %copy-done.2, f32[4,4096]{1,0:T(4,128)} %mid_ref.1, f32[4,4096]{1,0:T(4,128)} %copy-done.3, f32[128,128,128]{2,1,0:T(8,128)} %blk_ref.3), custom_call_target="tpu_custom_call" | custom-call | flops 16777216 | bytes 8650752 | tf_op jit(solution)/shard_map/pallas_call | solution.py:80
  16.8 13.8 %all_to_all.70 = f32[4,16,256]{2,0,1:T(4,128)S(1)} all-to-all(f32[4,16,256]{2,0,1:T(4,128)} %bitcast.21), channel_id=1, replica_groups=mesh['cells'=16,'tracer'=16] {'tracer'}, dimensions={1} | all-to-all | bytes 131072 | tf_op jit(solution)/shard_map/all_to_all | solution.py:120
  30.7 0.3 convolution_bitcast_fusion.1
  30.9 0.1 copy.12
  31.0 0.1 all_to_all.55
  31.1 10.8 %all_to_all.71 = f32[16,4,256]{2,1,0:T(4,128)S(1)} all-to-all(f32[16,4,256]{2,1,0:T(4,128)S(1)} %all_to_all.55), channel_id=1, replica_groups=mesh['cells'=16,'tracer'=16] {'tracer'}, dimensions={0} | all-to-all | bytes 131072 | tf_op jit(solution)/shard_map/all_to_all | solution.py:122
  41.9 0.0 copy-start.1
  41.9 0.1 collective-permute-start.3
  42.0 0.4 collective-permute-start.2
  42.4 1.5 %collective-permute-done.3.right_ref = f32[4,4096]{1,0:T(4,128)S(1)} collective-permute-done((f32[4,4096]{1,0:T(4,128)S(1)}, f32[4,4096]{1,0:T(4,128)S(1)}, u32[]{:S(2)}, u32[]{:S(2)}) %collective-permute-start.3) | collective-permute-done | bytes 65568 | tf_op jit(solution)/shard_map/ppermute | solution.py:101
  43.9 0.0 copy-start.4
  43.9 3.0 %collective-permute-done.2.left_ref = f32[4,4096]{1,0:T(4,128)S(1)} collective-permute-done((f32[4,4096]{1,0:T(4,128)S(1)}, f32[4,4096]{1,0:T(4,128)S(1)}, u32[]{:S(2)}, u32[]{:S(2)}) %collective-permute-start.2) | collective-permute-done | bytes 65568 | tf_op jit(solution)/shard_map/ppermute | solution.py:100
  46.9 0.0 copy-done.1
  46.9 0.0 copy-done.4
  46.9 0.0 copy-start.5
  46.9 0.6 copy-done.5
  47.5 8.7 %shard_map.65 = f32[4,4096]{1,0:T(4,128)} custom-call(s32[33]{0:T(128)} %bitcast.26, s32[128]{0:T(128)} %col_ref.3, f32[4,4096]{1,0:T(4,128)} %copy-done.5, f32[4,4096]{1,0:T(4,128)} %bitcast.19, f32[4,4096]{1,0:T(4,128)} %copy-done.4, f32[128,128,128]{2,1,0:T(8,128)} %blk_ref.3), custom_call_target="tpu_custom_call" | custom-call | flops 16777216 | bytes 8650752 | tf_op jit(solution)/shard_map/pallas_call | solution.py:80
  56.2 11.3 %all_to_all.72 = f32[4,16,256]{2,0,1:T(4,128)S(1)} all-to-all(f32[4,16,256]{2,0,1:T(4,128)} %bitcast.20), channel_id=1, replica_groups=mesh['cells'=16,'tracer'=16] {'tracer'}, dimensions={1} | all-to-all | bytes 131072 | tf_op jit(solution)/shard_map/all_to_all | solution.py:120
  67.6 0.3 convolution_bitcast_fusion
  67.9 0.1 copy.16
  67.9 0.1 all_to_all.62
  68.0 10.8 %all_to_all.73 = f32[16,4,256]{2,1,0:T(4,128)S(1)} all-to-all(f32[16,4,256]{2,1,0:T(4,128)S(1)} %all_to_all.62), channel_id=1, replica_groups=mesh['cells'=16,'tracer'=16] {'tracer'}, dimensions={0} | all-to-all | bytes 131072 | tf_op jit(solution)/shard_map/all_to_all | solution.py:122
  78.8 0.6 copy.24
  (3 shorter events, 0.1 us)
Async XLA Ops:
  0.0 6.1 %copy-start = (f32[8,64,64]{2,1,0:T(8,128)S(1)}, f32[8,64,64]{2,1,0:T(8,128)}, u32[]{:S(2)}) copy-start(f32[8,64,64]{2,1,0:T(8,128)} %param.11) | copy-start | bytes 393220
  0.0 7.5 %collective-permute-start = (f32[4,4096]{1,0:T(4,128)}, f32[4,4096]{1,0:T(4,128)S(1)}, u32[]{:S(2)}, u32[]{:S(2)}) collective-permute-start(f32[4,4096]{1,0:T(4,128)} %mid_ref.1), channel_id=1, source_target_pairs={{0,16},{16,32},{32,48},{48,64},{64,80},{80,96},{96,112},{112,128},... | collective-permute-start | bytes 196616 | tf_op jit(solution)/shard_map/ppermute | solution.py:100
  0.0 7.5 %collective-permute-start.1 = (f32[4,4096]{1,0:T(4,128)}, f32[4,4096]{1,0:T(4,128)S(1)}, u32[]{:S(2)}, u32[]{:S(2)}) collective-permute-start(f32[4,4096]{1,0:T(4,128)} %mid_ref.1), channel_id=1, source_target_pairs={{16,0},{32,16},{48,32},{64,48},{80,64},{96,80},{112,96},{128,112},... | collective-permute-start | bytes 196616 | tf_op jit(solution)/shard_map/ppermute | solution.py:101
  7.5 0.6 copy-start.2
  7.5 0.6 copy-start.3
  41.9 5.0 %copy-start.1 = (f32[16,4,256]{2,1,0:T(4,128)}, f32[16,4,256]{2,1,0:T(4,128)S(1)}, u32[]{:S(2)}) copy-start(f32[16,4,256]{2,1,0:T(4,128)S(1)} %all_to_all.71) | copy-start | bytes 196612
  41.9 2.0 %collective-permute-start.3 = (f32[4,4096]{1,0:T(4,128)S(1)}, f32[4,4096]{1,0:T(4,128)S(1)}, u32[]{:S(2)}, u32[]{:S(2)}) collective-permute-start(f32[4,4096]{1,0:T(4,128)S(1)} %bitcast.17), channel_id=1, source_target_pairs={{16,0},{32,16},{48,32},{64,48},{80,64},{96,80},{112,96},{128,112},... | collective-permute-start | bytes 196616 | tf_op jit(solution)/shard_map/ppermute | solution.py:101
  42.0 4.9 %collective-permute-start.2 = (f32[4,4096]{1,0:T(4,128)S(1)}, f32[4,4096]{1,0:T(4,128)S(1)}, u32[]{:S(2)}, u32[]{:S(2)}) collective-permute-start(f32[4,4096]{1,0:T(4,128)S(1)} %bitcast.18), channel_id=1, source_target_pairs={{0,16},{16,32},{32,48},{48,64},{64,80},{80,96},{96,112},{112,128},... | collective-permute-start | bytes 196616 | tf_op jit(solution)/shard_map/ppermute | solution.py:100
  43.9 3.0 %copy-start.4 = (f32[4,4096]{1,0:T(4,128)}, f32[4,4096]{1,0:T(4,128)S(1)}, u32[]{:S(2)}) copy-start(f32[4,4096]{1,0:T(4,128)S(1)} %collective-permute-done.3.right_ref) | copy-start | bytes 196612
  46.9 0.6 copy-start.5

commit v6 on v3

--- a/solution.py
+++ b/solution.py
@@ -95,6 +95,69 @@
     return out.reshape(spec, cells)
 
 
+def slot_kernel(rp_ref, col_ref, left_ref, mid_ref, right_ref, blk_ref, out_ref):
+    g = pl.program_id(0)
+    spec, cells = mid_ref.shape
+    nb_dev = cells // BLOCK
+    nb_total = nb_dev * lax.axis_size("cells")
+    first = (lax.axis_index("cells") - 1) * nb_dev
+    window = blk_ref.shape[0]
+    slots = col_ref.shape[0]
+    base = jnp.minimum(rp_ref[g * ROWS_PER_STEP], slots - window)
+    for rr in range(ROWS_PER_STEP):
+        r = g * ROWS_PER_STEP + rr
+        start = rp_ref[r]
+        cnt = rp_ref[r + 1] - start
+        off = start - base
+        for k in range(KMAX):
+            local = jnp.clip(off + k, 0, window - 1)
+            col = lax.rem(col_ref[base + local] - first + 2 * nb_total, nb_total)
+            col = jnp.clip(col, 0, 3 * nb_dev - 1)
+            piece = col // nb_dev
+            lane = pl.multiple_of((col - piece * nb_dev) * BLOCK, BLOCK)
+            x = jnp.where(
+                piece == 0,
+                left_ref[:, pl.ds(lane, BLOCK)],
+                jnp.where(piece == 1, mid_ref[:, pl.ds(lane, BLOCK)], right_ref[:, pl.ds(lane, BLOCK)]),
+            )
+            x = jnp.where(k < cnt, x, jnp.zeros_like(x))
+            out_ref[rr, k] = lax.dot_general(
+                x, blk_ref[local], (((1,), (1,)), ((), ())),
+                precision=lax.Precision.HIGHEST, preferred_element_type=jnp.float32,
+            )
+
+
+def transport_slots(left, mid, right, blocks, row_ptr, col_idx):
+    spec, cells = mid.shape
+    slots = blocks.shape[0]
+    nrows = row_ptr.shape[0] - 1
+    groups = nrows // ROWS_PER_STEP
+    window = ROWS_PER_STEP * KMAX
+    whole = lambda g, rp, ci: (0, 0)
+    grid_spec = pltpu.PrefetchScalarGridSpec(
+        num_scalar_prefetch=2,
+        grid=(groups,),
+        in_specs=[
+            pl.BlockSpec(mid.shape, whole),
+            pl.BlockSpec(mid.shape, whole),
+            pl.BlockSpec(mid.shape, whole),
+            pl.BlockSpec(
+                (pl.Element(window), pl.Element(BLOCK), pl.Element(BLOCK)),
+                lambda g, rp, ci: (jnp.minimum(rp[g * ROWS_PER_STEP], slots - window), 0, 0),
+            ),
+        ],
+        out_specs=pl.BlockSpec((ROWS_PER_STEP, KMAX, spec, BLOCK), lambda g, rp, ci: (g, 0, 0, 0)),
+    )
+    return pl.pallas_call(
+        slot_kernel,
+        grid_spec=grid_spec,
+        out_shape=jax.ShapeDtypeStruct((nrows, KMAX, spec, BLOCK), jnp.float32),
+        cost_estimate=pl.CostEstimate(
+            flops=2 * slots * BLOCK * BLOCK * spec, bytes_accessed=blocks.size * 4, transcendentals=0
+        ),
+    )(row_ptr, col_idx, left, mid, right, blocks)
+
+
 def halo(field):
     count = lax.axis_size("cells")
     left = lax.ppermute(field, "cells", [(i, (i + 1) % count) for i in range(count)])
@@ -105,20 +168,29 @@
 def body(adjoint, blocks, row_ptr, col_idx, regime, jac):
     spec_dev, cells_dev = adjoint.shape
     nb_dev = cells_dev // BLOCK
+    nb_total = nb_dev * lax.axis_size("cells")
+    cell_index = lax.axis_index("cells")
     tracer_devices = lax.axis_size("tracer")
     tracer_index = lax.axis_index("tracer")
     pointers = row_ptr.reshape(-1)
-    own_blocks = nb_dev // tracer_devices
-    own_regime = lax.dynamic_slice_in_dim(regime, tracer_index * own_blocks, own_blocks)
-    block_jac = jnp.take(jac, own_regime, axis=0)
-    adjoint_field = adjoint
-    for hour_step in range(STEPS):
-        left, right = halo(adjoint_field)
-        moved = transport(left, adjoint_field, right, blocks, pointers, col_idx)
-        split = lax.all_to_all(moved, "tracer", 1, 0, tiled=True)
-        reacted = chemistry_local(split, block_jac)
-        adjoint_field = lax.all_to_all(reacted, "tracer", 0, 1, tiled=True)
-    return adjoint_field
+    own_rows = nb_dev // tracer_devices
+    left, right = halo(adjoint)
+    moved = transport(left, adjoint, right, blocks, pointers, col_idx)
+    left, right = halo(moved)
+    per_slot = transport_slots(left, moved, right, blocks, pointers, col_idx)
+    split = lax.all_to_all(per_slot, "tracer", 0, 2, tiled=True)
+    reg_left, reg_right = halo(regime)
+    regime_ext = jnp.concatenate([reg_left, regime, reg_right])
+    rows = tracer_index * own_rows + jnp.arange(own_rows)
+    slot = jnp.minimum(pointers[rows][:, None] + jnp.arange(KMAX)[None, :], col_idx.shape[0] - 1)
+    local_col = jnp.mod(col_idx[slot] - (cell_index - 1) * nb_dev, nb_total)
+    local_col = jnp.clip(local_col, 0, 3 * nb_dev - 1)
+    jac_col = jnp.take(jac, regime_ext[local_col], axis=0)
+    jac_row = jnp.take(jac, regime[rows], axis=0)
+    combined = jnp.einsum("gkvu,gut->gkvt", jac_col, jac_row, precision=lax.Precision.HIGHEST)
+    reacted = jnp.einsum("gkvt,gkvc->tgc", combined, split, precision=lax.Precision.HIGHEST)
+    reacted = reacted.reshape(reacted.shape[0], own_rows * BLOCK)
+    return lax.all_to_all(reacted, "tracer", 0, 1, tiled=True)
 
 
 def solution(mesh):

time: 80.3 us -> 74.7 us (0.930)
  blocking collectives: 32.9 us -> 10.6 us
  Pallas kernels: 17.4 us -> 25.3 us
  local copies, waits for them, and re-layouts: 2.79 us -> 9.37 us
  starting transfers between devices: 13.3 us -> 18.7 us
  waiting for transfers between devices: 11.7 us -> 7.93 us
    all_to_all x3 -> x1, blocking collectives: 32.9 us -> 10.6 us  [body(): return lax.all_to_all(reacted, 'tracer', 0, 1, tiled=True)]
    pallas_call x0 -> x1, Pallas kernels: none -> 16.6 us  [transport_slots(): pl.pallas_call(slot_kernel, grid_spec=grid_spec, out_shape=jax.ShapeDtype...]
    pallas_call x2 -> x1, Pallas kernels: 17.4 us -> 8.68 us  [transport(): pl.pallas_call(transport_kernel, grid_spec=grid_spec, out_shape=jax.Shape...]
    ppermute x2 -> x3, starting transfers between devices: 5.42 us -> 11.2 us  [halo(): lax.ppermute(field, 'cells', [((i + 1) % count, i) for i in range(count)])]
    gather x1 -> x8, local copies, waits for them, and re-layouts: 0.55 us -> 5.81 us  [the longest x2 1.85 us: body(): jac_row = jnp.take(jac, regime[rows], axis=0)]
    ppermute x2 -> x3, waiting for transfers between devices: 4.4 us -> 2.07 us  [halo(): lax.ppermute(field, 'cells', [(i, (i + 1) % count) for i in range(count)])]
    ppermute x2 -> x3, waiting for transfers between devices: 1.59 us -> 0.07 us  [halo(): lax.ppermute(field, 'cells', [((i + 1) % count, i) for i in range(count)])]
    unnamed x13 -> x11, local copies, waits for them, and re-layouts: 1.9 us -> 3.07 us
  transfers between devices with their start and end apart: 5 -> 7, of which waited for: 5 -> 3; matrix products, arithmetic and copies ran while one was open for 2% -> 11% of each run, Pallas kernels for 0% -> 0%
where the time goes in v6:
time: 74.7 us; the launch traced here: 74.2 us
  Pallas kernels  25.3 us (34%)
  starting transfers between devices  18.7 us (25%)
  blocking collectives  10.6 us (14%)
  local copies, waits for them, and re-layouts  9.37 us (13%)
  waiting for transfers between devices  7.93 us (11%)
  matrix products  1.35 us (2%)
  other arithmetic  0.91 us (1%)
    pallas_call x1, Pallas kernels, transport_slots(): pl.pallas_call(slot_kernel, grid_spec=grid_spec, out_shape=jax.ShapeDtype...  16.6 us
    ppermute x3, starting transfers between devices, halo(): lax.ppermute(field, 'cells', [((i + 1) % count, i) for i in range(count)])  11.2 us
    all_to_all x1, blocking collectives, body(): return lax.all_to_all(reacted, 'tracer', 0, 1, tiled=True)  10.6 us
    pallas_call x1, Pallas kernels, transport(): pl.pallas_call(transport_kernel, grid_spec=grid_spec, out_shape=jax.Shape...  8.68 us
    all_to_all x1, starting transfers between devices, body(): split = lax.all_to_all(per_slot, 'tracer', 0, 2, tiled=True)  7.48 us
    all_to_all x1, waiting for transfers between devices, body(): split = lax.all_to_all(per_slot, 'tracer', 0, 2, tiled=True)  5.79 us
    unnamed x11, local copies, waits for them, and re-layouts  3.07 us
    ppermute x3, waiting for transfers between devices, halo(): lax.ppermute(field, 'cells', [(i, (i + 1) % count) for i in range(count)])  2.07 us
  transfers between devices with their start and end apart: 7, of which 3 were waited for; matrix products, arithmetic and copies ran while one was open for 11% of the time, Pallas kernels for 0%

profile of v6, /device:TPU:2, one launch (start us, length us, event | category | flops | bytes accessed | tf_op | source)
XLA Modules:
  0.0 74.2 jit_solution(16519077856155245349)
XLA Ops:
  0.0 0.0 copy-start
  0.0 0.0 collective-permute-start.4
  0.0 5.3 %collective-permute-start.5 = (s32[32]{0:T(128)}, s32[32]{0:T(128)S(1)}, u32[]{:S(2)}, u32[]{:S(2)}) collective-permute-start(s32[32]{0:T(128)} %param.10), channel_id=1, source_target_pairs={{16,0},{32,16},{48,32},{64,48},{80,64},{96,80},{112,96},{128,112},... | collective-permute-start | bytes 392 | tf_op jit(solution)/shard_map/ppermute | solution.py:164
  5.3 0.0 collective-permute-start
  5.3 3.0 %collective-permute-start.1 = (f32[4,4096]{1,0:T(4,128)}, f32[4,4096]{1,0:T(4,128)S(1)}, u32[]{:S(2)}, u32[]{:S(2)}) collective-permute-start(f32[4,4096]{1,0:T(4,128)} %mid_ref.1), channel_id=1, source_target_pairs={{16,0},{32,16},{48,32},{64,48},{80,64},{96,80},{112,96},{128,112},... | collective-permute-start | bytes 196616 | tf_op jit(solution)/shard_map/ppermute | solution.py:164
  8.3 1.3 %gather_fusion.4 = s32[2]{0:T(128)S(1)} fusion(s32[32]{0:T(128)} %param.10, s32[1024]{0:T(1024)S(1)} %pad_clamp_fusion.1), kind=kCustom, calls=%fused_computation.4 | custom fusion | bytes 24 | tf_op jit(solution)/shard_map/gather | solution.py:189
  9.6 1.3 %gather_fusion = s32[2]{0:T(128)S(1)} fusion(s32[33]{0:T(128)} %bitcast.35, s32[1024]{0:T(1024)S(1)} %pad_clamp_fusion.5), kind=kCustom, calls=%fused_computation | custom fusion | bytes 24 | tf_op jit(solution)/shard_map/gather | solution.py:185
  10.9 0.1 compare_select_fusion.3
  11.0 0.1 reshape.175
  11.1 1.3 %gather_fusion.1 = s32[8]{0:T(128)S(1)} fusion(s32[128]{0:T(128)} %col_ref.3, s32[1024]{0:T(1024)S(1)} %pad_clamp_fusion.4), kind=kCustom, calls=%fused_computation.1 | custom fusion | bytes 96 | tf_op jit(solution)/shard_map/gather | solution.py:186
  12.4 0.1 sub.22
  12.5 0.1 reshape.183
  12.6 0.0 copy-done
  12.6 0.6 gather_fusion.5
  13.2 0.0 collective-permute-done.4
  13.2 0.0 collective-permute-done.5
  13.2 0.7 pad_add_fusion
  13.9 0.6 gather_fusion.2
  14.6 0.1 gather.27
  14.7 0.1 reshape.182
  14.7 0.0 collective-permute-done.left_ref
  14.7 0.0 copy-start.1
  14.7 0.0 collective-permute-done.1.right_ref
  14.7 0.6 copy-done.1
  15.4 0.0 copy-start.2
  15.4 0.6 copy-done.2
  16.0 8.7 %shard_map.64.mid_ref = f32[4,4096]{1,0:T(4,128)} custom-call(s32[33]{0:T(128)} %bitcast.36, s32[128]{0:T(128)} %col_ref.3, f32[4,4096]{1,0:T(4,128)} %copy-done.1, f32[4,4096]{1,0:T(4,128)} %mid_ref.1, f32[4,4096]{1,0:T(4,128)} %copy-done.2, f32[128,128,128]{2,1,0:T(8,128)} %blk_ref.3), custom_call_target="tpu_custom_call" | custom-call | flops 16777216 | bytes 8650752 | tf_op jit(solution)/shard_map/pallas_call | solution.py:80
  24.7 0.0 collective-permute-start.2
  24.7 3.0 %collective-permute-start.3 = (f32[4,4096]{1,0:T(4,128)}, f32[4,4096]{1,0:T(4,128)S(1)}, u32[]{:S(2)}, u32[]{:S(2)}) collective-permute-start(f32[4,4096]{1,0:T(4,128)} %shard_map.64.mid_ref), channel_id=1, source_target_pairs={{16,0},{32,16},{48,32},{64,48},{80,64},{96,80},{112,96},{128,112},... | collective-permute-start | bytes 196616 | tf_op jit(solution)/shard_map/ppermute | solution.py:164
  27.6 0.1 reshape.191
  27.7 2.1 %collective-permute-done.2.left_ref = f32[4,4096]{1,0:T(4,128)S(1)} collective-permute-done((f32[4,4096]{1,0:T(4,128)}, f32[4,4096]{1,0:T(4,128)S(1)}, u32[]{:S(2)}, u32[]{:S(2)}) %collective-permute-start.2) | collective-permute-done | bytes 65568 | tf_op jit(solution)/shard_map/ppermute | solution.py:163
  29.8 0.0 copy-start.3
  29.8 0.1 collective-permute-done.3.right_ref
  29.9 0.6 copy-done.3
  30.4 0.0 copy-start.4
  30.4 0.6 copy-done.4
  31.0 16.6 %shard_map.65 = f32[32,4,4,128]{3,2,1,0:T(4,128)} custom-call(s32[33]{0:T(128)} %bitcast.37, s32[128]{0:T(128)} %col_ref.3, f32[4,4096]{1,0:T(4,128)} %copy-done.3, f32[4,4096]{1,0:T(4,128)} %shard_map.64.mid_ref, f32[4,4096]{1,0:T(4,128)} %copy-done.4, f32[128,128,128]{2,1,0:T(8,128)} %blk_ref.3), custom_call_target="tpu_custom_call" | custom-call | flops 16777216 | bytes 8388608 | tf_op jit(solution)/shard_map/pallas_call | solution.py:151
  47.6 7.5 %all-to-all-start = ((f32[32,4,4,128]{3,2,1,0:T(4,128)}), f32[32,4,4,128]{3,2,1,0:T(4,128)S(1)}, u32[]{:S(2)}, u32[]{:S(2)}) async-start(f32[32,4,4,128]{3,2,1,0:T(4,128)} %shard_map.65), calls=%async_computation | async-start | bytes 524288 | tf_op jit(solution)/shard_map/all_to_all | solution.py:181
  55.1 0.6 gather_fusion.3
  55.7 1.0 %fusion = f32[2,4,64,64]{2,3,1,0:T(8,128)S(1)} fusion(f32[2,4,64,64]{3,2,1,0:T(8,128)S(1)} %bitcast.39, pred[2,4]{1,0:T(4,128)(4,1)S(1)} %compare_and_fusion.1, f32[2,64,64]{2,1,0:T(8,128)S(1)} %gather_fusion.5, pred[2]{0:T(512)(128)(4,1)S(1)} %compare_and_fusion), kind=kOutput, calls=%fused_computation.7 | convolution fusion | flops 25206784 | bytes 294922 | tf_op jit(solution)/shard_map/gkvu,gut->gkvt/dot_general | solution.py:190
  56.7 5.8 %all-to-all-done = f32[32,4,4,128]{3,2,1,0:T(4,128)S(1)} async-done(((f32[32,4,4,128]{3,2,1,0:T(4,128)}), f32[32,4,4,128]{3,2,1,0:T(4,128)S(1)}, u32[]{:S(2)}, u32[]{:S(2)}) %all-to-all-start) | async-done | bytes 262176 | tf_op jit(solution)/shard_map/all_to_all | solution.py:181
  62.5 0.4 convolution_bitcast_fusion
  62.9 0.1 copy.9
  63.0 0.1 all_to_all.31
  63.0 10.6 %all_to_all.37 = f32[16,4,256]{2,1,0:T(4,128)S(1)} all-to-all(f32[16,4,256]{2,1,0:T(4,128)S(1)} %all_to_all.31), channel_id=1, replica_groups=mesh['cells'=16,'tracer'=16] {'tracer'}, dimensions={0} | all-to-all | bytes 131072 | tf_op jit(solution)/shard_map/all_to_all | solution.py:193
  73.6 0.6 copy.13
  (14 shorter events, 0.1 us)
Async XLA Ops:
  0.0 12.6 %copy-start = (f32[8,64,64]{2,1,0:T(8,128)S(1)}, f32[8,64,64]{2,1,0:T(8,128)}, u32[]{:S(2)}) copy-start(f32[8,64,64]{2,1,0:T(8,128)} %param.11) | copy-start | bytes 393220
  0.0 13.2 %collective-permute-start.4 = (s32[32]{0:T(128)}, s32[32]{0:T(128)S(1)}, u32[]{:S(2)}, u32[]{:S(2)}) collective-permute-start(s32[32]{0:T(128)} %param.10), channel_id=1, source_target_pairs={{0,16},{16,32},{32,48},{48,64},{64,80},{80,96},{96,112},{112,128},... | collective-permute-start | bytes 392 | tf_op jit(solution)/shard_map/ppermute | solution.py:163
  0.0 13.2 %collective-permute-start.5 = (s32[32]{0:T(128)}, s32[32]{0:T(128)S(1)}, u32[]{:S(2)}, u32[]{:S(2)}) collective-permute-start(s32[32]{0:T(128)} %param.10), channel_id=1, source_target_pairs={{16,0},{32,16},{48,32},{64,48},{80,64},{96,80},{112,96},{128,112},... | collective-permute-start | bytes 392 | tf_op jit(solution)/shard_map/ppermute | solution.py:164
  5.3 9.4 %collective-permute-start = (f32[4,4096]{1,0:T(4,128)}, f32[4,4096]{1,0:T(4,128)S(1)}, u32[]{:S(2)}, u32[]{:S(2)}) collective-permute-start(f32[4,4096]{1,0:T(4,128)} %mid_ref.1), channel_id=1, source_target_pairs={{0,16},{16,32},{32,48},{48,64},{64,80},{80,96},{96,112},{112,128},... | collective-permute-start | bytes 196616 | tf_op jit(solution)/shard_map/ppermute | solution.py:163
  5.3 9.4 %collective-permute-start.1 = (f32[4,4096]{1,0:T(4,128)}, f32[4,4096]{1,0:T(4,128)S(1)}, u32[]{:S(2)}, u32[]{:S(2)}) collective-permute-start(f32[4,4096]{1,0:T(4,128)} %mid_ref.1), channel_id=1, source_target_pairs={{16,0},{32,16},{48,32},{64,48},{80,64},{96,80},{112,96},{128,112},... | collective-permute-start | bytes 196616 | tf_op jit(solution)/shard_map/ppermute | solution.py:164
  14.7 0.6 copy-start.1
  15.4 0.6 copy-start.2
  24.7 5.1 %collective-permute-start.2 = (f32[4,4096]{1,0:T(4,128)}, f32[4,4096]{1,0:T(4,128)S(1)}, u32[]{:S(2)}, u32[]{:S(2)}) collective-permute-start(f32[4,4096]{1,0:T(4,128)} %shard_map.64.mid_ref), channel_id=1, source_target_pairs={{0,16},{16,32},{32,48},{48,64},{64,80},{80,96},{96,112},{112,128},... | collective-permute-start | bytes 196616 | tf_op jit(solution)/shard_map/ppermute | solution.py:163
  24.7 5.2 %collective-permute-start.3 = (f32[4,4096]{1,0:T(4,128)}, f32[4,4096]{1,0:T(4,128)S(1)}, u32[]{:S(2)}, u32[]{:S(2)}) collective-permute-start(f32[4,4096]{1,0:T(4,128)} %shard_map.64.mid_ref), channel_id=1, source_target_pairs={{16,0},{32,16},{48,32},{64,48},{80,64},{96,80},{112,96},{128,112},... | collective-permute-start | bytes 196616 | tf_op jit(solution)/shard_map/ppermute | solution.py:164
  29.8 0.6 copy-start.3
  30.4 0.6 copy-start.4
  47.6 14.8 %all-to-all-start = ((f32[32,4,4,128]{3,2,1,0:T(4,128)}), f32[32,4,4,128]{3,2,1,0:T(4,128)S(1)}, u32[]{:S(2)}, u32[]{:S(2)}) async-start(f32[32,4,4,128]{3,2,1,0:T(4,128)} %shard_map.65), calls=%async_computation | async-start | bytes 524288 | tf_op jit(solution)/shard_map/all_to_all | solution.py:181

commit v7 on v6

--- a/solution.py
+++ b/solution.py
@@ -34,8 +34,8 @@
             lane = pl.multiple_of((col - piece * nb_dev) * BLOCK, BLOCK)
             x = jnp.where(
                 piece == 0,
-                left_ref[:, pl.ds(lane, BLOCK)],
-                jnp.where(piece == 1, mid_ref[:, pl.ds(lane, BLOCK)], right_ref[:, pl.ds(lane, BLOCK)]),
+                left_ref[0:spec, pl.ds(lane, BLOCK)],
+                jnp.where(piece == 1, mid_ref[:, pl.ds(lane, BLOCK)], right_ref[0:spec, pl.ds(lane, BLOCK)]),
             )
             x = jnp.where(k < cnt, x, jnp.zeros_like(x))
             xs.append((local, x))
@@ -65,9 +65,9 @@
         num_scalar_prefetch=2,
         grid=(groups,),
         in_specs=[
-            pl.BlockSpec(mid.shape, whole),
-            pl.BlockSpec(mid.shape, whole),
-            pl.BlockSpec(mid.shape, whole),
+            pl.BlockSpec(left.shape, whole),
+            pl.BlockSpec(mid.shape, whole),
+            pl.BlockSpec(right.shape, whole),
             pl.BlockSpec(
                 (pl.Element(window), pl.Element(BLOCK), pl.Element(BLOCK)),
                 lambda g, rp, ci: (jnp.minimum(rp[g * ROWS_PER_STEP], slots - window), 0, 0),
@@ -158,6 +158,41 @@
     )(row_ptr, col_idx, left, mid, right, blocks)
 
 
+def combine_kernel(rp_ref, col_ref, reg_ref, jac_ref, out_ref):
+    own_rows = out_ref.shape[0]
+    slots = col_ref.shape[0]
+    nb_dev = reg_ref.shape[0] // 3
+    nb_total = nb_dev * lax.axis_size("cells")
+    first = (lax.axis_index("cells") - 1) * nb_dev
+    for g in range(own_rows):
+        row = lax.axis_index("tracer") * own_rows + g
+        nreg = jac_ref.shape[0]
+        row_jac = jac_ref[jnp.clip(reg_ref[nb_dev + row], 0, nreg - 1)]
+        for k in range(KMAX):
+            slot = jnp.minimum(rp_ref[row] + k, slots - 1)
+            col = lax.rem(col_ref[slot] - first + 2 * nb_total, nb_total)
+            col = jnp.clip(col, 0, 3 * nb_dev - 1)
+            out_ref[g, k] = jnp.dot(
+                jac_ref[jnp.clip(reg_ref[col], 0, nreg - 1)], row_jac,
+                precision=lax.Precision.HIGHEST, preferred_element_type=jnp.float32,
+            )
+
+
+def combined_jac(row_ptr, col_idx, regime_ext, jac, own_rows):
+    nreg, spec, _ = jac.shape
+    grid_spec = pltpu.PrefetchScalarGridSpec(
+        num_scalar_prefetch=3,
+        grid=(1,),
+        in_specs=[pl.BlockSpec(jac.shape, lambda i, rp, ci, rg: (0, 0, 0))],
+        out_specs=pl.BlockSpec((own_rows, KMAX, spec, spec), lambda i, rp, ci, rg: (0, 0, 0, 0)),
+    )
+    return pl.pallas_call(
+        combine_kernel,
+        grid_spec=grid_spec,
+        out_shape=jax.ShapeDtypeStruct((own_rows, KMAX, spec, spec), jnp.float32),
+    )(row_ptr, col_idx, regime_ext, jac)
+
+
 def halo(field):
     count = lax.axis_size("cells")
     left = lax.ppermute(field, "cells", [(i, (i + 1) % count) for i in range(count)])
@@ -174,20 +209,16 @@
     tracer_index = lax.axis_index("tracer")
     pointers = row_ptr.reshape(-1)
     own_rows = nb_dev // tracer_devices
-    left, right = halo(adjoint)
+    regime_row = jnp.zeros((1, cells_dev), jnp.float32).at[0, :nb_dev].set(regime.astype(jnp.float32))
+    left, right = halo(jnp.concatenate([adjoint, regime_row], axis=0))
     moved = transport(left, adjoint, right, blocks, pointers, col_idx)
+    regime_ext = jnp.concatenate(
+        [left[spec_dev, :nb_dev], regime_row[0, :nb_dev], right[spec_dev, :nb_dev]]
+    ).astype(jnp.int32)
     left, right = halo(moved)
     per_slot = transport_slots(left, moved, right, blocks, pointers, col_idx)
     split = lax.all_to_all(per_slot, "tracer", 0, 2, tiled=True)
-    reg_left, reg_right = halo(regime)
-    regime_ext = jnp.concatenate([reg_left, regime, reg_right])
-    rows = tracer_index * own_rows + jnp.arange(own_rows)
-    slot = jnp.minimum(pointers[rows][:, None] + jnp.arange(KMAX)[None, :], col_idx.shape[0] - 1)
-    local_col = jnp.mod(col_idx[slot] - (cell_index - 1) * nb_dev, nb_total)
-    local_col = jnp.clip(local_col, 0, 3 * nb_dev - 1)
-    jac_col = jnp.take(jac, regime_ext[local_col], axis=0)
-    jac_row = jnp.take(jac, regime[rows], axis=0)
-    combined = jnp.einsum("gkvu,gut->gkvt", jac_col, jac_row, precision=lax.Precision.HIGHEST)
+    combined = combined_jac(pointers, col_idx, regime_ext, jac, own_rows)
     reacted = jnp.einsum("gkvt,gkvc->tgc", combined, split, precision=lax.Precision.HIGHEST)
     reacted = reacted.reshape(reacted.shape[0], own_rows * BLOCK)
     return lax.all_to_all(reacted, "tracer", 0, 1, tiled=True)

time: 74.7 us -> 73.9 us (0.989)
  local copies, waits for them, and re-layouts: 9.37 us -> 3.42 us
  starting transfers between devices: 18.7 us -> 13.3 us
  other arithmetic: 0.91 us -> 4.69 us
  waiting for transfers between devices: 7.93 us -> 11.6 us
  Pallas kernels: 25.3 us -> 28 us
    ppermute x3 -> x2, starting transfers between devices: 11.2 us -> 5.36 us  [halo(): lax.ppermute(field, 'cells', [((i + 1) % count, i) for i in range(count)])]
    gather x8 -> x0, local copies, waits for them, and re-layouts: 5.81 us -> none  [the longest x2 1.85 us: body(): jac_row = jnp.take(jac, regime[rows], axis=0)]
    ppermute x3 -> x2, waiting for transfers between devices: 2.07 us -> 5.97 us  [halo(): lax.ppermute(field, 'cells', [(i, (i + 1) % count) for i in range(count)])]
    pallas_call x0 -> x1, Pallas kernels: none -> 2.69 us  [combined_jac(): pl.pallas_call(combine_kernel, grid_spec=grid_spec, out_shape=jax.ShapeDt...]
    all_to_all x1, waiting for transfers between devices: 5.79 us -> 3.37 us  [body(): split = lax.all_to_all(per_slot, 'tracer', 0, 2, tiled=True)]
    ppermute x3 -> x2, waiting for transfers between devices: 0.07 us -> 2.3 us  [halo(): lax.ppermute(field, 'cells', [((i + 1) % count, i) for i in range(count)])]
    squeeze x0 -> x2, local copies, waits for them, and re-layouts: none -> 1.35 us  [the longest x1 0.68 us: body(): left[spec_dev, :nb_dev]]
    squeeze x0 -> x1, other arithmetic: none -> 1.3 us  [body(): regime_row[0, :nb_dev]]
  transfers between devices with their start and end apart: 7 -> 5, of which waited for: 3 -> 5; matrix products, arithmetic and copies ran while one was open for 11% -> 4% of each run, Pallas kernels for 0% -> 4%
where the time goes in v7:
time: 73.9 us; the launch traced here: 73.3 us
  Pallas kernels  28 us (38%)
  starting transfers between devices  13.3 us (18%)
  waiting for transfers between devices  11.6 us (16%)
  blocking collectives  10.6 us (14%)
  other arithmetic  4.69 us (6%)
  local copies, waits for them, and re-layouts  3.42 us (5%)
  matrix products  1.56 us (2%)
    pallas_call x1, Pallas kernels, transport_slots(): pl.pallas_call(slot_kernel, grid_spec=grid_spec, out_shape=jax.ShapeDtype...  16.6 us
    all_to_all x1, blocking collectives, body(): return lax.all_to_all(reacted, 'tracer', 0, 1, tiled=True)  10.6 us
    pallas_call x1, Pallas kernels, transport(): pl.pallas_call(transport_kernel, grid_spec=grid_spec, out_shape=jax.Shape...  8.73 us
    all_to_all x1, starting transfers between devices, body(): split = lax.all_to_all(per_slot, 'tracer', 0, 2, tiled=True)  7.48 us
    ppermute x2, waiting for transfers between devices, halo(): lax.ppermute(field, 'cells', [(i, (i + 1) % count) for i in range(count)])  5.97 us
    ppermute x2, starting transfers between devices, halo(): lax.ppermute(field, 'cells', [((i + 1) % count, i) for i in range(count)])  5.36 us
    all_to_all x1, waiting for transfers between devices, body(): split = lax.all_to_all(per_slot, 'tracer', 0, 2, tiled=True)  3.37 us
    pallas_call x1, Pallas kernels, combined_jac(): pl.pallas_call(combine_kernel, grid_spec=grid_spec, out_shape=jax.ShapeDt...  2.69 us
  transfers between devices with their start and end apart: 5, of which 5 were waited for; matrix products, arithmetic and copies ran while one was open for 4% of the time, Pallas kernels for 4%

profile of v7, /device:TPU:2, one launch (start us, length us, event | category | flops | bytes accessed | tf_op | source)
XLA Modules:
  0.0 73.3 jit_solution(10602483285454239452)
XLA Ops:
  0.0 0.6 compare_reduce_fusion
  0.6 1.3 %fusion.2 = f32[1,32]{1,0:T(1,128)S(1)} fusion(s32[32]{0:T(128)} %param.12, pred[]{:T(512)} %compare_reduce_fusion), kind=kLoop, calls=%fused_computation.8 | loop fusion | flops 64 | bytes 257 | tf_op jit(solution)/shard_map/slice | solution.py:216
  1.9 0.9 %select_maximum_fusion = f32[5,4096]{1,0:T(8,128)S(1)} fusion(f32[1,32]{1,0:T(1,128)S(1)} %fusion.2, f32[4,4096]{1,0:T(4,128)} %mid_ref.1), kind=kLoop, calls=%fused_computation.1 | loop fusion | flops 61440 | bytes 147584 | tf_op jit(solution)/shard_map/concatenate | solution.py:213
  2.8 5.3 %collective-permute-start.1 = (f32[5,4096]{1,0:T(8,128)S(1)}, f32[5,4096]{1,0:T(8,128)S(1)}, u32[]{:S(2)}, u32[]{:S(2)}) collective-permute-start(f32[5,4096]{1,0:T(8,128)S(1)} %select_maximum_fusion), channel_id=1, source_target_pairs={{16,0},{32,16},{48,32},{64,48},{80,64},{96,80},{112,96},{128,112},... | collective-permute-start | bytes 245768 | tf_op jit(solution)/shard_map/ppermute | solution.py:199
  8.1 0.0 collective-permute-start
  8.1 1.3 %broadcast_select_fusion = f32[32]{0:T(128)S(1)} fusion(pred[]{:T(512)} %compare_reduce_fusion, s32[32]{0:T(128)} %param.12), kind=kLoop, calls=%fused_computation.4 | loop fusion | flops 64 | bytes 257 | tf_op jit(solution)/shard_map/squeeze | solution.py:216
  9.4 1.2 %collective-permute-done.1.right_ref = f32[5,4096]{1,0:T(8,128)S(1)} collective-permute-done((f32[5,4096]{1,0:T(8,128)S(1)}, f32[5,4096]{1,0:T(8,128)S(1)}, u32[]{:S(2)}, u32[]{:S(2)}) %collective-permute-start.1) | collective-permute-done | bytes 81952 | tf_op jit(solution)/shard_map/ppermute | solution.py:199
  10.6 0.0 copy-start.1
  10.6 3.1 %collective-permute-done.left_ref = f32[5,4096]{1,0:T(8,128)S(1)} collective-permute-done((f32[5,4096]{1,0:T(8,128)S(1)}, f32[5,4096]{1,0:T(8,128)S(1)}, u32[]{:S(2)}, u32[]{:S(2)}) %collective-permute-start) | collective-permute-done | bytes 81952 | tf_op jit(solution)/shard_map/ppermute | solution.py:198
  13.7 0.0 copy-start
  13.7 0.0 copy-done.1
  13.7 0.6 copy-done
  14.4 8.7 %shard_map.64.mid_ref = f32[4,4096]{1,0:T(4,128)} custom-call(s32[33]{0:T(128)} %bitcast.24, s32[128]{0:T(128)} %col_ref.5, f32[5,4096]{1,0:T(8,128)} %copy-done, f32[4,4096]{1,0:T(4,128)} %mid_ref.1, f32[5,4096]{1,0:T(8,128)} %copy-done.1, f32[128,128,128]{2,1,0:T(8,128)} %blk_ref.3), custom_call_target="tpu_custom_call" | custom-call | flops 16777216 | bytes 8650752 | tf_op jit(solution)/shard_map/pallas_call | solution.py:80
  23.1 0.1 collective-permute-start.3
  23.2 0.5 collective-permute-start.2
  23.6 0.7 slice_bitcast_fusion
  24.3 1.1 %collective-permute-done.3.right_ref = f32[4,4096]{1,0:T(4,128)S(1)} collective-permute-done((f32[4,4096]{1,0:T(4,128)}, f32[4,4096]{1,0:T(4,128)S(1)}, u32[]{:S(2)}, u32[]{:S(2)}) %collective-permute-start.3) | collective-permute-done | bytes 65568 | tf_op jit(solution)/shard_map/ppermute | solution.py:199
  25.4 0.0 copy-start.2
  25.4 2.9 %collective-permute-done.2.left_ref = f32[4,4096]{1,0:T(4,128)S(1)} collective-permute-done((f32[4,4096]{1,0:T(4,128)}, f32[4,4096]{1,0:T(4,128)S(1)}, u32[]{:S(2)}, u32[]{:S(2)}) %collective-permute-start.2) | collective-permute-done | bytes 65568 | tf_op jit(solution)/shard_map/ppermute | solution.py:198
  28.3 0.0 copy-done.2
  28.3 0.0 copy-start.3
  28.3 0.6 copy-done.3
  28.9 16.6 %shard_map.65 = f32[32,4,4,128]{3,2,1,0:T(4,128)} custom-call(s32[33]{0:T(128)} %bitcast.25, s32[128]{0:T(128)} %col_ref.5, f32[4,4096]{1,0:T(4,128)} %copy-done.3, f32[4,4096]{1,0:T(4,128)} %shard_map.64.mid_ref, f32[4,4096]{1,0:T(4,128)} %copy-done.2, f32[128,128,128]{2,1,0:T(8,128)} %blk_ref.3), custom_call_target="tpu_custom_call" | custom-call | flops 16777216 | bytes 8388608 | tf_op jit(solution)/shard_map/pallas_call | solution.py:151
  45.5 7.5 %all-to-all-start = ((f32[32,4,4,128]{3,2,1,0:T(4,128)}), f32[32,4,4,128]{3,2,1,0:T(4,128)S(1)}, u32[]{:S(2)}, u32[]{:S(2)}) async-start(f32[32,4,4,128]{3,2,1,0:T(4,128)} %shard_map.65), calls=%async_computation | async-start | bytes 524288 | tf_op jit(solution)/shard_map/all_to_all | solution.py:220
  53.0 0.7 slice_bitcast_fusion.1
  53.7 0.6 maximum_convert_fusion.reg_ref
  54.2 2.7 %shard_map.66 = f32[2,4,64,64]{3,2,1,0:T(8,128)} custom-call(s32[33]{0:T(128)} %bitcast.26, s32[128]{0:T(128)} %col_ref.5, s32[96]{0:T(128)} %maximum_convert_fusion.reg_ref, f32[8,64,64]{2,1,0:T(8,128)} %jac_ref.1), custom_call_target="tpu_custom_call" | custom-call | tf_op jit(solution)/shard_map/pallas_call | solution.py:189
  56.9 3.4 %all-to-all-done = f32[32,4,4,128]{3,2,1,0:T(4,128)S(1)} async-done(((f32[32,4,4,128]{3,2,1,0:T(4,128)}), f32[32,4,4,128]{3,2,1,0:T(4,128)S(1)}, u32[]{:S(2)}, u32[]{:S(2)}) %all-to-all-start) | async-done | bytes 262176 | tf_op jit(solution)/shard_map/all_to_all | solution.py:220
  60.4 1.6 %convolution_bitcast_fusion = f32[64,2,128]{2,0,1:T(8,128)S(1)} fusion(f32[2,4,64,128]{3,2,1,0:T(8,128)S(1)} %bitcast.22, f32[2,4,64,64]{3,2,1,0:T(8,128)} %shard_map.66), kind=kOutput, calls=%fused_computation | convolution fusion | flops 50331648 | bytes 458752 | tf_op jit(solution)/shard_map/gkvt,gkvc->tgc/dot_general | solution.py:222
  61.9 0.1 copy.11
  62.0 0.1 all_to_all.31
  62.1 10.6 %all_to_all.37 = f32[16,4,256]{2,1,0:T(4,128)S(1)} all-to-all(f32[16,4,256]{2,1,0:T(4,128)S(1)} %all_to_all.31), channel_id=1, replica_groups=mesh['cells'=16,'tracer'=16] {'tracer'}, dimensions={0} | all-to-all | bytes 131072 | tf_op jit(solution)/shard_map/all_to_all | solution.py:224
  72.6 0.6 copy.15
  (1 shorter events, 0.0 us)
Async XLA Ops:
  2.8 7.8 %collective-permute-start.1 = (f32[5,4096]{1,0:T(8,128)S(1)}, f32[5,4096]{1,0:T(8,128)S(1)}, u32[]{:S(2)}, u32[]{:S(2)}) collective-permute-start(f32[5,4096]{1,0:T(8,128)S(1)} %select_maximum_fusion), channel_id=1, source_target_pairs={{16,0},{32,16},{48,32},{64,48},{80,64},{96,80},{112,96},{128,112},... | collective-permute-start | bytes 245768 | tf_op jit(solution)/shard_map/ppermute | solution.py:199
  8.1 5.6 %collective-permute-start = (f32[5,4096]{1,0:T(8,128)S(1)}, f32[5,4096]{1,0:T(8,128)S(1)}, u32[]{:S(2)}, u32[]{:S(2)}) collective-permute-start(f32[5,4096]{1,0:T(8,128)S(1)} %select_maximum_fusion), channel_id=1, source_target_pairs={{0,16},{16,32},{32,48},{48,64},{64,80},{80,96},{96,112},{112,128},... | collective-permute-start | bytes 245768 | tf_op jit(solution)/shard_map/ppermute | solution.py:198
  10.6 3.1 %copy-start.1 = (f32[5,4096]{1,0:T(8,128)}, f32[5,4096]{1,0:T(8,128)S(1)}, u32[]{:S(2)}) copy-start(f32[5,4096]{1,0:T(8,128)S(1)} %collective-permute-done.1.right_ref) | copy-start | bytes 245764
  13.7 0.7 copy-start
  23.1 2.3 %collective-permute-start.3 = (f32[4,4096]{1,0:T(4,128)}, f32[4,4096]{1,0:T(4,128)S(1)}, u32[]{:S(2)}, u32[]{:S(2)}) collective-permute-start(f32[4,4096]{1,0:T(4,128)} %shard_map.64.mid_ref), channel_id=1, source_target_pairs={{16,0},{32,16},{48,32},{64,48},{80,64},{96,80},{112,96},{128,112},... | collective-permute-start | bytes 196616 | tf_op jit(solution)/shard_map/ppermute | solution.py:199
  23.2 5.1 %collective-permute-start.2 = (f32[4,4096]{1,0:T(4,128)}, f32[4,4096]{1,0:T(4,128)S(1)}, u32[]{:S(2)}, u32[]{:S(2)}) collective-permute-start(f32[4,4096]{1,0:T(4,128)} %shard_map.64.mid_ref), channel_id=1, source_target_pairs={{0,16},{16,32},{32,48},{48,64},{64,80},{80,96},{96,112},{112,128},... | collective-permute-start | bytes 196616 | tf_op jit(solution)/shard_map/ppermute | solution.py:198
  25.4 2.9 %copy-start.2 = (f32[4,4096]{1,0:T(4,128)}, f32[4,4096]{1,0:T(4,128)S(1)}, u32[]{:S(2)}) copy-start(f32[4,4096]{1,0:T(4,128)S(1)} %collective-permute-done.3.right_ref) | copy-start | bytes 196612
  28.3 0.6 copy-start.3
  45.5 14.8 %all-to-all-start = ((f32[32,4,4,128]{3,2,1,0:T(4,128)}), f32[32,4,4,128]{3,2,1,0:T(4,128)S(1)}, u32[]{:S(2)}, u32[]{:S(2)}) async-start(f32[32,4,4,128]{3,2,1,0:T(4,128)} %shard_map.65), calls=%async_computation | async-start | bytes 524288 | tf_op jit(solution)/shard_map/all_to_all | solution.py:220

commit v8 on v7

--- a/solution.py
+++ b/solution.py
@@ -11,7 +11,7 @@
 KMAX = 4
 
 
-def transport_kernel(rp_ref, col_ref, left_ref, mid_ref, right_ref, blk_ref, out_ref, acc_ref):
+def transport_kernel(rp_ref, col_ref, reg_ref, left_ref, mid_ref, right_ref, blk_ref, out_ref, acc_ref):
     g = pl.program_id(0)
     spec, cells = mid_ref.shape
     nb_dev = cells // BLOCK
@@ -52,17 +52,23 @@
         for q in range(spec):
             y = jnp.sum(acc_ref[q].T, axis=0, keepdims=True)
             out_ref[q:q + 1, rr * BLOCK:(rr + 1) * BLOCK] = y
-
-
-def transport(left, mid, right, blocks, row_ptr, col_idx):
+    width = out_ref.shape[1]
+    lane = lax.broadcasted_iota(jnp.int32, (1, width), 1) + g * width
+    tag = jnp.zeros((1, width), jnp.float32)
+    for i in range(reg_ref.shape[0]):
+        tag = jnp.where(lane == i, reg_ref[i].astype(jnp.float32), tag)
+    out_ref[spec:spec + 1, :] = tag
+
+
+def transport(left, mid, right, blocks, row_ptr, col_idx, regime):
     spec, cells = mid.shape
     slots = blocks.shape[0]
     nrows = row_ptr.shape[0] - 1
     groups = nrows // ROWS_PER_STEP
     window = ROWS_PER_STEP * KMAX
-    whole = lambda g, rp, ci: (0, 0)
+    whole = lambda g, rp, ci, rg: (0, 0)
     grid_spec = pltpu.PrefetchScalarGridSpec(
-        num_scalar_prefetch=2,
+        num_scalar_prefetch=3,
         grid=(groups,),
         in_specs=[
             pl.BlockSpec(left.shape, whole),
@@ -70,21 +76,21 @@
             pl.BlockSpec(right.shape, whole),
             pl.BlockSpec(
                 (pl.Element(window), pl.Element(BLOCK), pl.Element(BLOCK)),
-                lambda g, rp, ci: (jnp.minimum(rp[g * ROWS_PER_STEP], slots - window), 0, 0),
+                lambda g, rp, ci, rg: (jnp.minimum(rp[g * ROWS_PER_STEP], slots - window), 0, 0),
             ),
         ],
-        out_specs=pl.BlockSpec((spec, ROWS_PER_STEP * BLOCK), lambda g, rp, ci: (0, g)),
+        out_specs=pl.BlockSpec((spec + 1, ROWS_PER_STEP * BLOCK), lambda g, rp, ci, rg: (0, g)),
         scratch_shapes=[pltpu.VMEM((spec, BLOCK, BLOCK), jnp.float32)],
     )
     flops = 2 * slots * BLOCK * BLOCK * spec
     return pl.pallas_call(
         transport_kernel,
         grid_spec=grid_spec,
-        out_shape=jax.ShapeDtypeStruct((spec, nrows * BLOCK), jnp.float32),
+        out_shape=jax.ShapeDtypeStruct((spec + 1, nrows * BLOCK), jnp.float32),
         cost_estimate=pl.CostEstimate(
             flops=flops, bytes_accessed=blocks.size * 4 + 4 * mid.size * 4, transcendentals=0
         ),
-    )(row_ptr, col_idx, left, mid, right, blocks)
+    )(row_ptr, col_idx, regime, left, mid, right, blocks)
 
 
 def chemistry_local(moved, block_jac):
@@ -97,8 +103,8 @@
 
 def slot_kernel(rp_ref, col_ref, left_ref, mid_ref, right_ref, blk_ref, out_ref):
     g = pl.program_id(0)
-    spec, cells = mid_ref.shape
-    nb_dev = cells // BLOCK
+    spec = out_ref.shape[2]
+    nb_dev = mid_ref.shape[1] // BLOCK
     nb_total = nb_dev * lax.axis_size("cells")
     first = (lax.axis_index("cells") - 1) * nb_dev
     window = blk_ref.shape[0]
@@ -117,8 +123,8 @@
             lane = pl.multiple_of((col - piece * nb_dev) * BLOCK, BLOCK)
             x = jnp.where(
                 piece == 0,
-                left_ref[:, pl.ds(lane, BLOCK)],
-                jnp.where(piece == 1, mid_ref[:, pl.ds(lane, BLOCK)], right_ref[:, pl.ds(lane, BLOCK)]),
+                left_ref[0:spec, pl.ds(lane, BLOCK)],
+                jnp.where(piece == 1, mid_ref[0:spec, pl.ds(lane, BLOCK)], right_ref[0:spec, pl.ds(lane, BLOCK)]),
             )
             x = jnp.where(k < cnt, x, jnp.zeros_like(x))
             out_ref[rr, k] = lax.dot_general(
@@ -128,7 +134,7 @@
 
 
 def transport_slots(left, mid, right, blocks, row_ptr, col_idx):
-    spec, cells = mid.shape
+    spec = mid.shape[0] - 1
     slots = blocks.shape[0]
     nrows = row_ptr.shape[0] - 1
     groups = nrows // ROWS_PER_STEP
@@ -209,14 +215,13 @@
     tracer_index = lax.axis_index("tracer")
     pointers = row_ptr.reshape(-1)
     own_rows = nb_dev // tracer_devices
-    regime_row = jnp.zeros((1, cells_dev), jnp.float32).at[0, :nb_dev].set(regime.astype(jnp.float32))
-    left, right = halo(jnp.concatenate([adjoint, regime_row], axis=0))
-    moved = transport(left, adjoint, right, blocks, pointers, col_idx)
-    regime_ext = jnp.concatenate(
-        [left[spec_dev, :nb_dev], regime_row[0, :nb_dev], right[spec_dev, :nb_dev]]
-    ).astype(jnp.int32)
+    left, right = halo(adjoint)
+    moved = transport(left, adjoint, right, blocks, pointers, col_idx, regime)
     left, right = halo(moved)
     per_slot = transport_slots(left, moved, right, blocks, pointers, col_idx)
+    regime_ext = jnp.concatenate(
+        [left[spec_dev, :nb_dev], moved[spec_dev, :nb_dev], right[spec_dev, :nb_dev]]
+    ).astype(jnp.int32)
     split = lax.all_to_all(per_slot, "tracer", 0, 2, tiled=True)
     combined = combined_jac(pointers, col_idx, regime_ext, jac, own_rows)
     reacted = jnp.einsum("gkvt,gkvc->tgc", combined, split, precision=lax.Precision.HIGHEST)

time: 73.9 us -> 71.3 us (0.965)
  other arithmetic: 4.69 us -> 0.59 us
  starting transfers between devices: 13.3 us -> 15.7 us
  waiting for transfers between devices: 11.6 us -> 10 us
    ppermute x2, starting transfers between devices: 5.36 us -> 8.19 us  [halo(): lax.ppermute(field, 'cells', [((i + 1) % count, i) for i in range(count)])]
    squeeze x1 -> x0, other arithmetic: 1.3 us -> none  [body(): regime_row[0, :nb_dev]]
    slice x1 -> x0, other arithmetic: 1.3 us -> none  [body(): regime_row[0, :nb_dev]]
    concatenate x1 -> x0, other arithmetic: 0.85 us -> none  [body(): left, right = halo(jnp.concatenate([adjoint, regime_row], axis=0))]
    ppermute x2, waiting for transfers between devices: 5.97 us -> 5.13 us  [halo(): lax.ppermute(field, 'cells', [(i, (i + 1) % count) for i in range(count)])]
where the time goes in v8:
time: 71.3 us; the launch traced here: 70.7 us
  Pallas kernels  28.1 us (39%)
  starting transfers between devices  15.7 us (22%)
  blocking collectives  10.6 us (15%)
  waiting for transfers between devices  10 us (14%)
  local copies, waits for them, and re-layouts  4.14 us (6%)
  matrix products  1.56 us (2%)
    pallas_call x1, Pallas kernels, transport_slots(): pl.pallas_call(slot_kernel, grid_spec=grid_spec, out_shape=jax.ShapeDtype...  16.7 us
    all_to_all x1, blocking collectives, body(): return lax.all_to_all(reacted, 'tracer', 0, 1, tiled=True)  10.6 us
    pallas_call x1, Pallas kernels, transport(): pl.pallas_call(transport_kernel, grid_spec=grid_spec, out_shape=jax.Shape...  8.7 us
    ppermute x2, starting transfers between devices, halo(): lax.ppermute(field, 'cells', [((i + 1) % count, i) for i in range(count)])  8.19 us
    all_to_all x1, starting transfers between devices, body(): split = lax.all_to_all(per_slot, 'tracer', 0, 2, tiled=True)  7.48 us
    ppermute x2, waiting for transfers between devices, halo(): lax.ppermute(field, 'cells', [(i, (i + 1) % count) for i in range(count)])  5.13 us
    pallas_call x1, Pallas kernels, combined_jac(): pl.pallas_call(combine_kernel, grid_spec=grid_spec, out_shape=jax.ShapeDt...  2.7 us
    all_to_all x1, waiting for transfers between devices, body(): split = lax.all_to_all(per_slot, 'tracer', 0, 2, tiled=True)  2.68 us
  transfers between devices with their start and end apart: 5, of which 5 were waited for; matrix products, arithmetic and copies ran while one was open for 4% of the time, Pallas kernels for 4%

profile of v8, /device:TPU:2, one launch (start us, length us, event | category | flops | bytes accessed | tf_op | source)
XLA Modules:
  0.0 70.7 jit_solution(1664047250363287539)
XLA Ops:
  0.0 0.0 collective-permute-start
  0.0 5.3 %collective-permute-start.1 = (f32[4,4096]{1,0:T(4,128)}, f32[4,4096]{1,0:T(4,128)S(1)}, u32[]{:S(2)}, u32[]{:S(2)}) collective-permute-start(f32[4,4096]{1,0:T(4,128)} %mid_ref.1), channel_id=1, source_target_pairs={{16,0},{32,16},{48,32},{64,48},{80,64},{96,80},{112,96},{128,112},... | collective-permute-start | bytes 196616 | tf_op jit(solution)/shard_map/ppermute | solution.py:205
  5.3 2.2 %collective-permute-done.left_ref = f32[4,4096]{1,0:T(4,128)S(1)} collective-permute-done((f32[4,4096]{1,0:T(4,128)}, f32[4,4096]{1,0:T(4,128)S(1)}, u32[]{:S(2)}, u32[]{:S(2)}) %collective-permute-start) | collective-permute-done | bytes 65568 | tf_op jit(solution)/shard_map/ppermute | solution.py:204
  7.5 0.0 copy-start.2
  7.5 0.1 collective-permute-done.1.right_ref
  7.5 0.0 copy-start.3
  7.5 0.6 copy-done.2
  8.1 0.1 copy-done.3
  8.1 8.7 %shard_map.64.mid_ref = f32[5,4096]{1,0:T(8,128)} custom-call(s32[33]{0:T(128)} %bitcast.24, s32[128]{0:T(128)} %col_ref.5, s32[32]{0:T(128)} %reg_ref.1, f32[4,4096]{1,0:T(4,128)} %copy-done.2, f32[4,4096]{1,0:T(4,128)} %mid_ref.1, f32[4,4096]{1,0:T(4,128)} %copy-done.3, f32[128,128,128]{2,1,0:T(8,128)} %blk_ref.3), custom_call_target="tpu_custom_call" | custom-call | flops 16777216 | bytes 8650752 | tf_op jit(solution)/shard_map/pallas_call | solution.py:86
  16.8 2.9 %collective-permute-start.3 = (f32[5,4096]{1,0:T(8,128)}, f32[5,4096]{1,0:T(8,128)S(1)}, u32[]{:S(2)}, u32[]{:S(2)}) collective-permute-start(f32[5,4096]{1,0:T(8,128)} %shard_map.64.mid_ref), channel_id=1, source_target_pairs={{16,0},{32,16},{48,32},{64,48},{80,64},{96,80},{112,96},{128,112},... | collective-permute-start | bytes 245768 | tf_op jit(solution)/shard_map/ppermute | solution.py:205
  19.7 0.0 collective-permute-start.2
  19.7 0.7 %slice_bitcast_fusion.1 = f32[32]{0:T(128)S(1)} fusion(f32[5,4096]{1,0:T(8,128)} %shard_map.64.mid_ref), kind=kLoop, calls=%fused_computation.2 | loop fusion | bytes 256 | tf_op jit(solution)/shard_map/squeeze | solution.py:223
  20.5 2.1 %collective-permute-done.3.right_ref = f32[5,4096]{1,0:T(8,128)S(1)} collective-permute-done((f32[5,4096]{1,0:T(8,128)}, f32[5,4096]{1,0:T(8,128)S(1)}, u32[]{:S(2)}, u32[]{:S(2)}) %collective-permute-start.3) | collective-permute-done | bytes 81952 | tf_op jit(solution)/shard_map/ppermute | solution.py:205
  22.6 0.0 copy-start
  22.6 3.0 %collective-permute-done.2.left_ref = f32[5,4096]{1,0:T(8,128)S(1)} collective-permute-done((f32[5,4096]{1,0:T(8,128)}, f32[5,4096]{1,0:T(8,128)S(1)}, u32[]{:S(2)}, u32[]{:S(2)}) %collective-permute-start.2) | collective-permute-done | bytes 81952 | tf_op jit(solution)/shard_map/ppermute | solution.py:204
  25.6 0.0 copy-done
  25.6 0.0 copy-start.1
  25.6 0.7 copy-done.1
  26.2 16.7 %shard_map.65 = f32[32,4,4,128]{3,2,1,0:T(4,128)} custom-call(s32[33]{0:T(128)} %bitcast.25, s32[128]{0:T(128)} %col_ref.5, f32[5,4096]{1,0:T(8,128)} %copy-done.1, f32[5,4096]{1,0:T(8,128)} %shard_map.64.mid_ref, f32[5,4096]{1,0:T(8,128)} %copy-done, f32[128,128,128]{2,1,0:T(8,128)} %blk_ref.3), custom_call_target="tpu_custom_call" | custom-call | flops 16777216 | bytes 8388608 | tf_op jit(solution)/shard_map/pallas_call | solution.py:157
  42.9 7.5 %all-to-all-start = ((f32[32,4,4,128]{3,2,1,0:T(4,128)}), f32[32,4,4,128]{3,2,1,0:T(4,128)S(1)}, u32[]{:S(2)}, u32[]{:S(2)}) async-start(f32[32,4,4,128]{3,2,1,0:T(4,128)} %shard_map.65), calls=%async_computation | async-start | bytes 524288 | tf_op jit(solution)/shard_map/all_to_all | solution.py:225
  50.4 0.7 slice_bitcast_fusion
  51.0 0.7 slice_bitcast_fusion.2
  51.7 0.6 maximum_convert_fusion.reg_ref
  52.3 2.7 %shard_map.66 = f32[2,4,64,64]{3,2,1,0:T(8,128)} custom-call(s32[33]{0:T(128)} %bitcast.26, s32[128]{0:T(128)} %col_ref.5, s32[96]{0:T(128)} %maximum_convert_fusion.reg_ref, f32[8,64,64]{2,1,0:T(8,128)} %jac_ref.1), custom_call_target="tpu_custom_call" | custom-call | tf_op jit(solution)/shard_map/pallas_call | solution.py:195
  55.0 2.7 %all-to-all-done = f32[32,4,4,128]{3,2,1,0:T(4,128)S(1)} async-done(((f32[32,4,4,128]{3,2,1,0:T(4,128)}), f32[32,4,4,128]{3,2,1,0:T(4,128)S(1)}, u32[]{:S(2)}, u32[]{:S(2)}) %all-to-all-start) | async-done | bytes 262176 | tf_op jit(solution)/shard_map/all_to_all | solution.py:225
  57.7 1.6 %convolution_bitcast_fusion = f32[64,2,128]{2,0,1:T(8,128)S(1)} fusion(f32[2,4,64,128]{3,2,1,0:T(8,128)S(1)} %bitcast.22, f32[2,4,64,64]{3,2,1,0:T(8,128)} %shard_map.66), kind=kOutput, calls=%fused_computation | convolution fusion | flops 50331648 | bytes 458752 | tf_op jit(solution)/shard_map/gkvt,gkvc->tgc/dot_general | solution.py:227
  59.3 0.1 copy.11
  59.4 0.1 all_to_all.31
  59.4 10.6 %all_to_all.37 = f32[16,4,256]{2,1,0:T(4,128)S(1)} all-to-all(f32[16,4,256]{2,1,0:T(4,128)S(1)} %all_to_all.31), channel_id=1, replica_groups=mesh['cells'=16,'tracer'=16] {'tracer'}, dimensions={0} | all-to-all | bytes 131072 | tf_op jit(solution)/shard_map/all_to_all | solution.py:229
  70.1 0.6 copy.15
  (1 shorter events, 0.0 us)
Async XLA Ops:
  0.0 7.5 %collective-permute-start = (f32[4,4096]{1,0:T(4,128)}, f32[4,4096]{1,0:T(4,128)S(1)}, u32[]{:S(2)}, u32[]{:S(2)}) collective-permute-start(f32[4,4096]{1,0:T(4,128)} %mid_ref.1), channel_id=1, source_target_pairs={{0,16},{16,32},{32,48},{48,64},{64,80},{80,96},{96,112},{112,128},... | collective-permute-start | bytes 196616 | tf_op jit(solution)/shard_map/ppermute | solution.py:204
  0.0 7.5 %collective-permute-start.1 = (f32[4,4096]{1,0:T(4,128)}, f32[4,4096]{1,0:T(4,128)S(1)}, u32[]{:S(2)}, u32[]{:S(2)}) collective-permute-start(f32[4,4096]{1,0:T(4,128)} %mid_ref.1), channel_id=1, source_target_pairs={{16,0},{32,16},{48,32},{64,48},{80,64},{96,80},{112,96},{128,112},... | collective-permute-start | bytes 196616 | tf_op jit(solution)/shard_map/ppermute | solution.py:205
  7.5 0.6 copy-start.2
  7.5 0.6 copy-start.3
  16.8 5.7 %collective-permute-start.3 = (f32[5,4096]{1,0:T(8,128)}, f32[5,4096]{1,0:T(8,128)S(1)}, u32[]{:S(2)}, u32[]{:S(2)}) collective-permute-start(f32[5,4096]{1,0:T(8,128)} %shard_map.64.mid_ref), channel_id=1, source_target_pairs={{16,0},{32,16},{48,32},{64,48},{80,64},{96,80},{112,96},{128,112},... | collective-permute-start | bytes 245768 | tf_op jit(solution)/shard_map/ppermute | solution.py:205
  19.7 5.8 %collective-permute-start.2 = (f32[5,4096]{1,0:T(8,128)}, f32[5,4096]{1,0:T(8,128)S(1)}, u32[]{:S(2)}, u32[]{:S(2)}) collective-permute-start(f32[5,4096]{1,0:T(8,128)} %shard_map.64.mid_ref), channel_id=1, source_target_pairs={{0,16},{16,32},{32,48},{48,64},{64,80},{80,96},{96,112},{112,128},... | collective-permute-start | bytes 245768 | tf_op jit(solution)/shard_map/ppermute | solution.py:204
  22.6 3.0 %copy-start = (f32[5,4096]{1,0:T(8,128)}, f32[5,4096]{1,0:T(8,128)S(1)}, u32[]{:S(2)}) copy-start(f32[5,4096]{1,0:T(8,128)S(1)} %collective-permute-done.3.right_ref) | copy-start | bytes 245764
  25.6 0.7 copy-start.1
  42.9 14.8 %all-to-all-start = ((f32[32,4,4,128]{3,2,1,0:T(4,128)}), f32[32,4,4,128]{3,2,1,0:T(4,128)S(1)}, u32[]{:S(2)}, u32[]{:S(2)}) async-start(f32[32,4,4,128]{3,2,1,0:T(4,128)} %shard_map.65), calls=%async_computation | async-start | bytes 524288 | tf_op jit(solution)/shard_map/all_to_all | solution.py:225

commit v9 on v8

--- a/solution.py
+++ b/solution.py
@@ -129,7 +129,7 @@
             x = jnp.where(k < cnt, x, jnp.zeros_like(x))
             out_ref[rr, k] = lax.dot_general(
                 x, blk_ref[local], (((1,), (1,)), ((), ())),
-                precision=lax.Precision.HIGHEST, preferred_element_type=jnp.float32,
+                precision=lax.Precision.HIGH, preferred_element_type=jnp.float32,
             )
 
 

time: 71.3 us -> 66 us (0.926)
  Pallas kernels: 28.1 us -> 22.6 us
    pallas_call x1, Pallas kernels: 16.7 us -> 11.2 us  [transport_slots(): pl.pallas_call(slot_kernel, grid_spec=grid_spec, out_shape=jax.ShapeDtype...]
where the time goes in v9:
time: 66 us; the launch traced here: 65.2 us
  Pallas kernels  22.6 us (34%)
  starting transfers between devices  15.7 us (24%)
  blocking collectives  10.6 us (16%)
  waiting for transfers between devices  10 us (15%)
  local copies, waits for them, and re-layouts  4.14 us (6%)
  matrix products  1.56 us (2%)
    pallas_call x1, Pallas kernels, transport_slots(): pl.pallas_call(slot_kernel, grid_spec=grid_spec, out_shape=jax.ShapeDtype...  11.2 us
    all_to_all x1, blocking collectives, body(): return lax.all_to_all(reacted, 'tracer', 0, 1, tiled=True)  10.6 us
    pallas_call x1, Pallas kernels, transport(): pl.pallas_call(transport_kernel, grid_spec=grid_spec, out_shape=jax.Shape...  8.71 us
    ppermute x2, starting transfers between devices, halo(): lax.ppermute(field, 'cells', [((i + 1) % count, i) for i in range(count)])  8.19 us
    all_to_all x1, starting transfers between devices, body(): split = lax.all_to_all(per_slot, 'tracer', 0, 2, tiled=True)  7.48 us
    ppermute x2, waiting for transfers between devices, halo(): lax.ppermute(field, 'cells', [(i, (i + 1) % count) for i in range(count)])  5.13 us
    pallas_call x1, Pallas kernels, combined_jac(): pl.pallas_call(combine_kernel, grid_spec=grid_spec, out_shape=jax.ShapeDt...  2.7 us
    all_to_all x1, waiting for transfers between devices, body(): split = lax.all_to_all(per_slot, 'tracer', 0, 2, tiled=True)  2.68 us
  transfers between devices with their start and end apart: 5, of which 5 were waited for; matrix products, arithmetic and copies ran while one was open for 4% of the time, Pallas kernels for 4%

profile of v9, /device:TPU:2, one launch (start us, length us, event | category | flops | bytes accessed | tf_op | source)
XLA Modules:
  0.0 65.2 jit_solution(9802197316291336947)
XLA Ops:
  0.0 0.0 collective-permute-start
  0.0 5.3 %collective-permute-start.1 = (f32[4,4096]{1,0:T(4,128)}, f32[4,4096]{1,0:T(4,128)S(1)}, u32[]{:S(2)}, u32[]{:S(2)}) collective-permute-start(f32[4,4096]{1,0:T(4,128)} %mid_ref.1), channel_id=1, source_target_pairs={{16,0},{32,16},{48,32},{64,48},{80,64},{96,80},{112,96},{128,112},... | collective-permute-start | bytes 196616 | tf_op jit(solution)/shard_map/ppermute | solution.py:205
  5.3 2.2 %collective-permute-done.left_ref = f32[4,4096]{1,0:T(4,128)S(1)} collective-permute-done((f32[4,4096]{1,0:T(4,128)}, f32[4,4096]{1,0:T(4,128)S(1)}, u32[]{:S(2)}, u32[]{:S(2)}) %collective-permute-start) | collective-permute-done | bytes 65568 | tf_op jit(solution)/shard_map/ppermute | solution.py:204
  7.5 0.0 copy-start.2
  7.5 0.1 collective-permute-done.1.right_ref
  7.5 0.0 copy-start.3
  7.5 0.6 copy-done.2
  8.1 0.1 copy-done.3
  8.1 8.7 %shard_map.64.mid_ref = f32[5,4096]{1,0:T(8,128)} custom-call(s32[33]{0:T(128)} %bitcast.24, s32[128]{0:T(128)} %col_ref.5, s32[32]{0:T(128)} %reg_ref.1, f32[4,4096]{1,0:T(4,128)} %copy-done.2, f32[4,4096]{1,0:T(4,128)} %mid_ref.1, f32[4,4096]{1,0:T(4,128)} %copy-done.3, f32[128,128,128]{2,1,0:T(8,128)} %blk_ref.3), custom_call_target="tpu_custom_call" | custom-call | flops 16777216 | bytes 8650752 | tf_op jit(solution)/shard_map/pallas_call | solution.py:86
  16.8 2.9 %collective-permute-start.3 = (f32[5,4096]{1,0:T(8,128)}, f32[5,4096]{1,0:T(8,128)S(1)}, u32[]{:S(2)}, u32[]{:S(2)}) collective-permute-start(f32[5,4096]{1,0:T(8,128)} %shard_map.64.mid_ref), channel_id=1, source_target_pairs={{16,0},{32,16},{48,32},{64,48},{80,64},{96,80},{112,96},{128,112},... | collective-permute-start | bytes 245768 | tf_op jit(solution)/shard_map/ppermute | solution.py:205
  19.7 0.0 collective-permute-start.2
  19.7 0.7 %slice_bitcast_fusion.1 = f32[32]{0:T(128)S(1)} fusion(f32[5,4096]{1,0:T(8,128)} %shard_map.64.mid_ref), kind=kLoop, calls=%fused_computation.2 | loop fusion | bytes 256 | tf_op jit(solution)/shard_map/squeeze | solution.py:223
  20.5 2.1 %collective-permute-done.3.right_ref = f32[5,4096]{1,0:T(8,128)S(1)} collective-permute-done((f32[5,4096]{1,0:T(8,128)}, f32[5,4096]{1,0:T(8,128)S(1)}, u32[]{:S(2)}, u32[]{:S(2)}) %collective-permute-start.3) | collective-permute-done | bytes 81952 | tf_op jit(solution)/shard_map/ppermute | solution.py:205
  22.6 0.0 copy-start
  22.6 3.0 %collective-permute-done.2.left_ref = f32[5,4096]{1,0:T(8,128)S(1)} collective-permute-done((f32[5,4096]{1,0:T(8,128)}, f32[5,4096]{1,0:T(8,128)S(1)}, u32[]{:S(2)}, u32[]{:S(2)}) %collective-permute-start.2) | collective-permute-done | bytes 81952 | tf_op jit(solution)/shard_map/ppermute | solution.py:204
  25.6 0.0 copy-done
  25.6 0.0 copy-start.1
  25.6 0.7 copy-done.1
  26.2 11.2 %shard_map.65 = f32[32,4,4,128]{3,2,1,0:T(4,128)} custom-call(s32[33]{0:T(128)} %bitcast.25, s32[128]{0:T(128)} %col_ref.5, f32[5,4096]{1,0:T(8,128)} %copy-done.1, f32[5,4096]{1,0:T(8,128)} %shard_map.64.mid_ref, f32[5,4096]{1,0:T(8,128)} %copy-done, f32[128,128,128]{2,1,0:T(8,128)} %blk_ref.3), custom_call_target="tpu_custom_call" | custom-call | flops 16777216 | bytes 8388608 | tf_op jit(solution)/shard_map/pallas_call | solution.py:157
  37.4 7.5 %all-to-all-start = ((f32[32,4,4,128]{3,2,1,0:T(4,128)}), f32[32,4,4,128]{3,2,1,0:T(4,128)S(1)}, u32[]{:S(2)}, u32[]{:S(2)}) async-start(f32[32,4,4,128]{3,2,1,0:T(4,128)} %shard_map.65), calls=%async_computation | async-start | bytes 524288 | tf_op jit(solution)/shard_map/all_to_all | solution.py:225
  44.9 0.7 %slice_bitcast_fusion = f32[32]{0:T(128)S(1)} fusion(f32[5,4096]{1,0:T(8,128)} %copy-done), kind=kLoop, calls=%fused_computation.1 | loop fusion | bytes 256 | tf_op jit(solution)/shard_map/squeeze | solution.py:223
  45.6 0.7 %slice_bitcast_fusion.2 = f32[32]{0:T(128)S(1)} fusion(f32[5,4096]{1,0:T(8,128)} %copy-done.1), kind=kLoop, calls=%fused_computation.3 | loop fusion | bytes 256 | tf_op jit(solution)/shard_map/squeeze | solution.py:223
  46.2 0.6 maximum_convert_fusion.reg_ref
  46.8 2.7 %shard_map.66 = f32[2,4,64,64]{3,2,1,0:T(8,128)} custom-call(s32[33]{0:T(128)} %bitcast.26, s32[128]{0:T(128)} %col_ref.5, s32[96]{0:T(128)} %maximum_convert_fusion.reg_ref, f32[8,64,64]{2,1,0:T(8,128)} %jac_ref.1), custom_call_target="tpu_custom_call" | custom-call | tf_op jit(solution)/shard_map/pallas_call | solution.py:195
  49.5 2.7 %all-to-all-done = f32[32,4,4,128]{3,2,1,0:T(4,128)S(1)} async-done(((f32[32,4,4,128]{3,2,1,0:T(4,128)}), f32[32,4,4,128]{3,2,1,0:T(4,128)S(1)}, u32[]{:S(2)}, u32[]{:S(2)}) %all-to-all-start) | async-done | bytes 262176 | tf_op jit(solution)/shard_map/all_to_all | solution.py:225
  52.3 1.6 %convolution_bitcast_fusion = f32[64,2,128]{2,0,1:T(8,128)S(1)} fusion(f32[2,4,64,128]{3,2,1,0:T(8,128)S(1)} %bitcast.22, f32[2,4,64,64]{3,2,1,0:T(8,128)} %shard_map.66), kind=kOutput, calls=%fused_computation | convolution fusion | flops 50331648 | bytes 458752 | tf_op jit(solution)/shard_map/gkvt,gkvc->tgc/dot_general | solution.py:227
  53.8 0.1 copy.11
  53.9 0.1 all_to_all.31
  54.0 10.6 %all_to_all.37 = f32[16,4,256]{2,1,0:T(4,128)S(1)} all-to-all(f32[16,4,256]{2,1,0:T(4,128)S(1)} %all_to_all.31), channel_id=1, replica_groups=mesh['cells'=16,'tracer'=16] {'tracer'}, dimensions={0} | all-to-all | bytes 131072 | tf_op jit(solution)/shard_map/all_to_all | solution.py:229
  64.6 0.6 copy.15
  (1 shorter events, 0.0 us)
Async XLA Ops:
  0.0 7.5 %collective-permute-start = (f32[4,4096]{1,0:T(4,128)}, f32[4,4096]{1,0:T(4,128)S(1)}, u32[]{:S(2)}, u32[]{:S(2)}) collective-permute-start(f32[4,4096]{1,0:T(4,128)} %mid_ref.1), channel_id=1, source_target_pairs={{0,16},{16,32},{32,48},{48,64},{64,80},{80,96},{96,112},{112,128},... | collective-permute-start | bytes 196616 | tf_op jit(solution)/shard_map/ppermute | solution.py:204
  0.0 7.5 %collective-permute-start.1 = (f32[4,4096]{1,0:T(4,128)}, f32[4,4096]{1,0:T(4,128)S(1)}, u32[]{:S(2)}, u32[]{:S(2)}) collective-permute-start(f32[4,4096]{1,0:T(4,128)} %mid_ref.1), channel_id=1, source_target_pairs={{16,0},{32,16},{48,32},{64,48},{80,64},{96,80},{112,96},{128,112},... | collective-permute-start | bytes 196616 | tf_op jit(solution)/shard_map/ppermute | solution.py:205
  7.5 0.6 copy-start.2
  7.5 0.6 copy-start.3
  16.8 5.7 %collective-permute-start.3 = (f32[5,4096]{1,0:T(8,128)}, f32[5,4096]{1,0:T(8,128)S(1)}, u32[]{:S(2)}, u32[]{:S(2)}) collective-permute-start(f32[5,4096]{1,0:T(8,128)} %shard_map.64.mid_ref), channel_id=1, source_target_pairs={{16,0},{32,16},{48,32},{64,48},{80,64},{96,80},{112,96},{128,112},... | collective-permute-start | bytes 245768 | tf_op jit(solution)/shard_map/ppermute | solution.py:205
  19.7 5.8 %collective-permute-start.2 = (f32[5,4096]{1,0:T(8,128)}, f32[5,4096]{1,0:T(8,128)S(1)}, u32[]{:S(2)}, u32[]{:S(2)}) collective-permute-start(f32[5,4096]{1,0:T(8,128)} %shard_map.64.mid_ref), channel_id=1, source_target_pairs={{0,16},{16,32},{32,48},{48,64},{64,80},{80,96},{96,112},{112,128},... | collective-permute-start | bytes 245768 | tf_op jit(solution)/shard_map/ppermute | solution.py:204
  22.6 3.0 %copy-start = (f32[5,4096]{1,0:T(8,128)}, f32[5,4096]{1,0:T(8,128)S(1)}, u32[]{:S(2)}) copy-start(f32[5,4096]{1,0:T(8,128)S(1)} %collective-permute-done.3.right_ref) | copy-start | bytes 245764
  25.6 0.7 copy-start.1
  37.4 14.8 %all-to-all-start = ((f32[32,4,4,128]{3,2,1,0:T(4,128)}), f32[32,4,4,128]{3,2,1,0:T(4,128)S(1)}, u32[]{:S(2)}, u32[]{:S(2)}) async-start(f32[32,4,4,128]{3,2,1,0:T(4,128)} %shard_map.65), calls=%async_computation | async-start | bytes 524288 | tf_op jit(solution)/shard_map/all_to_all | solution.py:225

commit v10 on v9

--- a/solution.py
+++ b/solution.py
@@ -7,7 +7,7 @@
 
 BLOCK = 128
 STEPS = 2
-ROWS_PER_STEP = 4
+ROWS_PER_STEP = 8
 KMAX = 4
 
 

time: 66 us -> 62.7 us (0.950)
  Pallas kernels: 22.6 us -> 19.6 us
    pallas_call x1, Pallas kernels: 8.71 us -> 6.92 us  [transport(): pl.pallas_call(transport_kernel, grid_spec=grid_spec, out_shape=jax.Shape...]
    pallas_call x1, Pallas kernels: 11.2 us -> 9.97 us  [transport_slots(): pl.pallas_call(slot_kernel, grid_spec=grid_spec, out_shape=jax.ShapeDtype...]
where the time goes in v10:
time: 62.7 us; the launch traced here: 62.2 us
  Pallas kernels  19.6 us (31%)
  starting transfers between devices  15.7 us (25%)
  blocking collectives  10.6 us (17%)
  waiting for transfers between devices  10 us (16%)
  local copies, waits for them, and re-layouts  4.14 us (7%)
  matrix products  1.56 us (2%)
    all_to_all x1, blocking collectives, body(): return lax.all_to_all(reacted, 'tracer', 0, 1, tiled=True)  10.6 us
    pallas_call x1, Pallas kernels, transport_slots(): pl.pallas_call(slot_kernel, grid_spec=grid_spec, out_shape=jax.ShapeDtype...  9.97 us
    ppermute x2, starting transfers between devices, halo(): lax.ppermute(field, 'cells', [((i + 1) % count, i) for i in range(count)])  8.19 us
    all_to_all x1, starting transfers between devices, body(): split = lax.all_to_all(per_slot, 'tracer', 0, 2, tiled=True)  7.48 us
    pallas_call x1, Pallas kernels, transport(): pl.pallas_call(transport_kernel, grid_spec=grid_spec, out_shape=jax.Shape...  6.92 us
    ppermute x2, waiting for transfers between devices, halo(): lax.ppermute(field, 'cells', [(i, (i + 1) % count) for i in range(count)])  5.13 us
    pallas_call x1, Pallas kernels, combined_jac(): pl.pallas_call(combine_kernel, grid_spec=grid_spec, out_shape=jax.ShapeDt...  2.7 us
    all_to_all x1, waiting for transfers between devices, body(): split = lax.all_to_all(per_slot, 'tracer', 0, 2, tiled=True)  2.68 us
  transfers between devices with their start and end apart: 5, of which 5 were waited for; matrix products, arithmetic and copies ran while one was open for 4% of the time, Pallas kernels for 4%

profile of v10, /device:TPU:2, one launch (start us, length us, event | category | flops | bytes accessed | tf_op | source)
XLA Modules:
  0.0 62.2 jit_solution(6044474245015315124)
XLA Ops:
  0.0 0.0 collective-permute-start
  0.0 5.3 %collective-permute-start.1 = (f32[4,4096]{1,0:T(4,128)}, f32[4,4096]{1,0:T(4,128)S(1)}, u32[]{:S(2)}, u32[]{:S(2)}) collective-permute-start(f32[4,4096]{1,0:T(4,128)} %mid_ref.1), channel_id=1, source_target_pairs={{16,0},{32,16},{48,32},{64,48},{80,64},{96,80},{112,96},{128,112},... | collective-permute-start | bytes 196616 | tf_op jit(solution)/shard_map/ppermute | solution.py:205
  5.3 2.2 %collective-permute-done.left_ref = f32[4,4096]{1,0:T(4,128)S(1)} collective-permute-done((f32[4,4096]{1,0:T(4,128)}, f32[4,4096]{1,0:T(4,128)S(1)}, u32[]{:S(2)}, u32[]{:S(2)}) %collective-permute-start) | collective-permute-done | bytes 65568 | tf_op jit(solution)/shard_map/ppermute | solution.py:204
  7.5 0.0 copy-start.2
  7.5 0.1 collective-permute-done.1.right_ref
  7.5 0.0 copy-start.3
  7.5 0.6 copy-done.2
  8.1 0.1 copy-done.3
  8.1 6.9 %shard_map.64.mid_ref = f32[5,4096]{1,0:T(8,128)} custom-call(s32[33]{0:T(128)} %bitcast.24, s32[128]{0:T(128)} %col_ref.5, s32[32]{0:T(128)} %reg_ref.1, f32[4,4096]{1,0:T(4,128)} %copy-done.2, f32[4,4096]{1,0:T(4,128)} %mid_ref.1, f32[4,4096]{1,0:T(4,128)} %copy-done.3, f32[128,128,128]{2,1,0:T(8,128)} %blk_ref.3), custom_call_target="tpu_custom_call" | custom-call | flops 16777216 | bytes 8650752 | tf_op jit(solution)/shard_map/pallas_call | solution.py:86
  15.1 2.9 %collective-permute-start.3 = (f32[5,4096]{1,0:T(8,128)}, f32[5,4096]{1,0:T(8,128)S(1)}, u32[]{:S(2)}, u32[]{:S(2)}) collective-permute-start(f32[5,4096]{1,0:T(8,128)} %shard_map.64.mid_ref), channel_id=1, source_target_pairs={{16,0},{32,16},{48,32},{64,48},{80,64},{96,80},{112,96},{128,112},... | collective-permute-start | bytes 245768 | tf_op jit(solution)/shard_map/ppermute | solution.py:205
  18.0 0.0 collective-permute-start.2
  18.0 0.7 %slice_bitcast_fusion.1 = f32[32]{0:T(128)S(1)} fusion(f32[5,4096]{1,0:T(8,128)} %shard_map.64.mid_ref), kind=kLoop, calls=%fused_computation.2 | loop fusion | bytes 256 | tf_op jit(solution)/shard_map/squeeze | solution.py:223
  18.7 2.1 %collective-permute-done.3.right_ref = f32[5,4096]{1,0:T(8,128)S(1)} collective-permute-done((f32[5,4096]{1,0:T(8,128)}, f32[5,4096]{1,0:T(8,128)S(1)}, u32[]{:S(2)}, u32[]{:S(2)}) %collective-permute-start.3) | collective-permute-done | bytes 81952 | tf_op jit(solution)/shard_map/ppermute | solution.py:205
  20.8 0.0 copy-start
  20.8 3.0 %collective-permute-done.2.left_ref = f32[5,4096]{1,0:T(8,128)S(1)} collective-permute-done((f32[5,4096]{1,0:T(8,128)}, f32[5,4096]{1,0:T(8,128)S(1)}, u32[]{:S(2)}, u32[]{:S(2)}) %collective-permute-start.2) | collective-permute-done | bytes 81952 | tf_op jit(solution)/shard_map/ppermute | solution.py:204
  23.8 0.0 copy-done
  23.8 0.0 copy-start.1
  23.8 0.7 %copy-done.1 = f32[5,4096]{1,0:T(8,128)} copy-done((f32[5,4096]{1,0:T(8,128)}, f32[5,4096]{1,0:T(8,128)S(1)}, u32[]{:S(2)}) %copy-start.1) | copy-done | bytes 81944
  24.4 10.0 %shard_map.65 = f32[32,4,4,128]{3,2,1,0:T(4,128)} custom-call(s32[33]{0:T(128)} %bitcast.25, s32[128]{0:T(128)} %col_ref.5, f32[5,4096]{1,0:T(8,128)} %copy-done.1, f32[5,4096]{1,0:T(8,128)} %shard_map.64.mid_ref, f32[5,4096]{1,0:T(8,128)} %copy-done, f32[128,128,128]{2,1,0:T(8,128)} %blk_ref.3), custom_call_target="tpu_custom_call" | custom-call | flops 16777216 | bytes 8388608 | tf_op jit(solution)/shard_map/pallas_call | solution.py:157
  34.4 7.5 %all-to-all-start = ((f32[32,4,4,128]{3,2,1,0:T(4,128)}), f32[32,4,4,128]{3,2,1,0:T(4,128)S(1)}, u32[]{:S(2)}, u32[]{:S(2)}) async-start(f32[32,4,4,128]{3,2,1,0:T(4,128)} %shard_map.65), calls=%async_computation | async-start | bytes 524288 | tf_op jit(solution)/shard_map/all_to_all | solution.py:225
  41.9 0.7 %slice_bitcast_fusion = f32[32]{0:T(128)S(1)} fusion(f32[5,4096]{1,0:T(8,128)} %copy-done), kind=kLoop, calls=%fused_computation.1 | loop fusion | bytes 256 | tf_op jit(solution)/shard_map/squeeze | solution.py:223
  42.5 0.7 %slice_bitcast_fusion.2 = f32[32]{0:T(128)S(1)} fusion(f32[5,4096]{1,0:T(8,128)} %copy-done.1), kind=kLoop, calls=%fused_computation.3 | loop fusion | bytes 256 | tf_op jit(solution)/shard_map/squeeze | solution.py:223
  43.2 0.6 maximum_convert_fusion.reg_ref
  43.8 2.7 %shard_map.66 = f32[2,4,64,64]{3,2,1,0:T(8,128)} custom-call(s32[33]{0:T(128)} %bitcast.26, s32[128]{0:T(128)} %col_ref.5, s32[96]{0:T(128)} %maximum_convert_fusion.reg_ref, f32[8,64,64]{2,1,0:T(8,128)} %jac_ref.1), custom_call_target="tpu_custom_call" | custom-call | tf_op jit(solution)/shard_map/pallas_call | solution.py:195
  46.5 2.7 %all-to-all-done = f32[32,4,4,128]{3,2,1,0:T(4,128)S(1)} async-done(((f32[32,4,4,128]{3,2,1,0:T(4,128)}), f32[32,4,4,128]{3,2,1,0:T(4,128)S(1)}, u32[]{:S(2)}, u32[]{:S(2)}) %all-to-all-start) | async-done | bytes 262176 | tf_op jit(solution)/shard_map/all_to_all | solution.py:225
  49.3 1.6 %convolution_bitcast_fusion = f32[64,2,128]{2,0,1:T(8,128)S(1)} fusion(f32[2,4,64,128]{3,2,1,0:T(8,128)S(1)} %bitcast.22, f32[2,4,64,64]{3,2,1,0:T(8,128)} %shard_map.66), kind=kOutput, calls=%fused_computation | convolution fusion | flops 50331648 | bytes 458752 | tf_op jit(solution)/shard_map/gkvt,gkvc->tgc/dot_general | solution.py:227
  50.8 0.1 copy.11
  50.9 0.1 all_to_all.31
  51.0 10.6 %all_to_all.37 = f32[16,4,256]{2,1,0:T(4,128)S(1)} all-to-all(f32[16,4,256]{2,1,0:T(4,128)S(1)} %all_to_all.31), channel_id=1, replica_groups=mesh['cells'=16,'tracer'=16] {'tracer'}, dimensions={0} | all-to-all | bytes 131072 | tf_op jit(solution)/shard_map/all_to_all | solution.py:229
  61.6 0.6 %copy.15 = f32[4,4096]{1,0:T(4,128)} copy(f32[4,4096]{1,0:T(4,128)S(1)} %bitcast.23) | data formatting | bytes 131072
  (1 shorter events, 0.0 us)
Async XLA Ops:
  0.0 7.5 %collective-permute-start = (f32[4,4096]{1,0:T(4,128)}, f32[4,4096]{1,0:T(4,128)S(1)}, u32[]{:S(2)}, u32[]{:S(2)}) collective-permute-start(f32[4,4096]{1,0:T(4,128)} %mid_ref.1), channel_id=1, source_target_pairs={{0,16},{16,32},{32,48},{48,64},{64,80},{80,96},{96,112},{112,128},... | collective-permute-start | bytes 196616 | tf_op jit(solution)/shard_map/ppermute | solution.py:204
  0.0 7.5 %collective-permute-start.1 = (f32[4,4096]{1,0:T(4,128)}, f32[4,4096]{1,0:T(4,128)S(1)}, u32[]{:S(2)}, u32[]{:S(2)}) collective-permute-start(f32[4,4096]{1,0:T(4,128)} %mid_ref.1), channel_id=1, source_target_pairs={{16,0},{32,16},{48,32},{64,48},{80,64},{96,80},{112,96},{128,112},... | collective-permute-start | bytes 196616 | tf_op jit(solution)/shard_map/ppermute | solution.py:205
  7.5 0.6 %copy-start.2 = (f32[4,4096]{1,0:T(4,128)}, f32[4,4096]{1,0:T(4,128)S(1)}, u32[]{:S(2)}) copy-start(f32[4,4096]{1,0:T(4,128)S(1)} %collective-permute-done.left_ref) | copy-start | bytes 196612
  7.5 0.6 copy-start.3
  15.1 5.7 %collective-permute-start.3 = (f32[5,4096]{1,0:T(8,128)}, f32[5,4096]{1,0:T(8,128)S(1)}, u32[]{:S(2)}, u32[]{:S(2)}) collective-permute-start(f32[5,4096]{1,0:T(8,128)} %shard_map.64.mid_ref), channel_id=1, source_target_pairs={{16,0},{32,16},{48,32},{64,48},{80,64},{96,80},{112,96},{128,112},... | collective-permute-start | bytes 245768 | tf_op jit(solution)/shard_map/ppermute | solution.py:205
  18.0 5.8 %collective-permute-start.2 = (f32[5,4096]{1,0:T(8,128)}, f32[5,4096]{1,0:T(8,128)S(1)}, u32[]{:S(2)}, u32[]{:S(2)}) collective-permute-start(f32[5,4096]{1,0:T(8,128)} %shard_map.64.mid_ref), channel_id=1, source_target_pairs={{0,16},{16,32},{32,48},{48,64},{64,80},{80,96},{96,112},{112,128},... | collective-permute-start | bytes 245768 | tf_op jit(solution)/shard_map/ppermute | solution.py:204
  20.8 3.0 %copy-start = (f32[5,4096]{1,0:T(8,128)}, f32[5,4096]{1,0:T(8,128)S(1)}, u32[]{:S(2)}) copy-start(f32[5,4096]{1,0:T(8,128)S(1)} %collective-permute-done.3.right_ref) | copy-start | bytes 245764
  23.8 0.7 %copy-start.1 = (f32[5,4096]{1,0:T(8,128)}, f32[5,4096]{1,0:T(8,128)S(1)}, u32[]{:S(2)}) copy-start(f32[5,4096]{1,0:T(8,128)S(1)} %collective-permute-done.2.left_ref) | copy-start | bytes 245764
  34.4 14.8 %all-to-all-start = ((f32[32,4,4,128]{3,2,1,0:T(4,128)}), f32[32,4,4,128]{3,2,1,0:T(4,128)S(1)}, u32[]{:S(2)}, u32[]{:S(2)}) async-start(f32[32,4,4,128]{3,2,1,0:T(4,128)} %shard_map.65), calls=%async_computation | async-start | bytes 524288 | tf_op jit(solution)/shard_map/all_to_all | solution.py:225
